TPU v7x, 256 devices: a whole 4x4x8 slice. The times are simulated.
256 devices in a mesh: blk: 32 (over z, x_lo, core), col: 8 (over x_hi, y).
Axes of the slice: x: 4 (x_hi: 2, x_lo: 2; x = x_hi * 2 + x_lo), y: 4, z: 8, core: 2. Of those that a mesh axis runs over, the one named last changes fastest.
Arguments:
- feat1: bfloat16 [128, 384, 256], P('blk', 'col'), may hold values from -40 to 40
- feat2: bfloat16 [128, 384, 256], P('blk', 'col'), may hold values from -40 to 40
Outputs:
- flow: float32 [2, 128, 384], P(None, 'blk', 'col')
- grad_flow: float32 [2, 128, 384], P(None, 'blk', 'col')
- grad_warped: float32 [128, 384, 256], P('blk', 'col')
All inputs are finite; a program needn't handle non-finite values.
Results may differ from a plain program's by a relative error of at most 0.0075.
Values may be sent and summed in bfloat16 or wider, within the bound.
No kernel may reach another device: no remote copies, remote signals or barrier semaphores. Data moves between devices by JAX's collectives and lax.ppermute only.
A program may use at most 64 MiB of HBM per device.

v0:
```python
import math

import jax
import jax.numpy as jnp
from jax import lax
from jax.sharding import PartitionSpec as P

ssim_one = 0.01
ssim_two = 0.03
charb_sq = 0.0001


def with_halo(value, sides, width):
    for axis, dim in sides:
        count, length = (lax.axis_size(axis), value.shape[dim])
        up = [(i, (i + 1) % count) for i in range(count - 1)]
        down = [(j, i) for i, j in up]
        last = lax.slice_in_dim(value, length - width, length, axis=dim)
        first = lax.slice_in_dim(value, 0, width, axis=dim)
        before = lax.ppermute(last, axis, up)
        after = lax.ppermute(first, axis, down)
        value = jnp.concatenate([before, value, after], axis=dim)
    return value


def box_valid(padded):
    rows_out = padded.shape[0] - 2
    cols_out = padded.shape[1] - 2
    total = jnp.zeros((rows_out, cols_out) + padded.shape[2:], padded.dtype)
    for offset_r in range(3):
        for offset_c in range(3):
            total = total + padded[offset_r : offset_r + rows_out, offset_c : offset_c + cols_out]
    return total / 9.0


def ssim_loss(mean_y, var_y, cov_xy, mean_x, var_x):
    top = (2.0 * mean_x * mean_y + ssim_one) * (2.0 * cov_xy + ssim_two)
    bottom = (mean_x * mean_x + mean_y * mean_y + ssim_one) * (var_x + var_y + ssim_two)
    return jnp.sum((1.0 - top / bottom) * 0.5)


def local_terms(xpad, ypad):
    mean_x = box_valid(xpad)
    mean_y = box_valid(ypad)
    var_x = box_valid(xpad * xpad) - mean_x * mean_x
    var_y = box_valid(ypad * ypad) - mean_y * mean_y
    cov_xy = box_valid(xpad * ypad) - mean_x * mean_y
    loss, pull = jax.vjp(
        lambda one, two, three: ssim_loss(one, two, three, mean_x, var_x), mean_y, var_y, cov_xy
    )
    grad_mean, grad_var, grad_cov = pull(jnp.ones_like(loss))
    first = grad_mean - 2.0 * grad_var * mean_y - grad_cov * mean_x
    return (first, grad_var, grad_cov)


def edge_weight(lower, upper):
    return jnp.exp(-jnp.mean(jnp.abs(upper - lower), axis=-1))


def charbonnier(weight, delta):
    return weight * delta / jnp.sqrt(delta * delta + charb_sq)


def absorb(carry, queries, keys, key_y, key_x, scale):
    total_keys = keys.shape[0]
    width = keys.shape[1]
    step = min(total_keys, 2048)
    while total_keys % step != 0:
        step = step - 1
    blocks = total_keys // step

    def visit(state, item):
        top, total, acc, along_y, along_x = state
        key_block, block_y, block_x = item
        score = (
            lax.dot_general(
                queries, key_block, (((1,), (1,)), ((), ())), preferred_element_type=jnp.float32
            )
            * scale
        )
        new_top = jnp.maximum(top, jnp.max(score, axis=1))
        shrink = jnp.exp(top - new_top)
        expo = jnp.exp(score - new_top[:, None])
        total = total * shrink + jnp.sum(expo, axis=1)
        acc = acc * shrink[:, None] + jnp.dot(
            expo.astype(jnp.bfloat16), key_block, preferred_element_type=jnp.float32
        )
        along_y = along_y * shrink + jnp.sum(expo * block_y[None, :], axis=1)
        along_x = along_x * shrink + jnp.sum(expo * block_x[None, :], axis=1)
        return ((new_top, total, acc, along_y, along_x), None)

    items = (
        keys.reshape(blocks, step, width),
        key_y.reshape(blocks, step),
        key_x.reshape(blocks, step),
    )
    carry, unused = lax.scan(visit, carry, items)
    return carry


def body(feat1, feat2):
    rows, cols, width = feat1.shape
    ncol = lax.axis_size("col")
    full_rows = rows * lax.axis_size("blk")
    full_cols = cols * ncol
    row_start = lax.axis_index("blk") * rows
    col_start = lax.axis_index("col") * cols
    scale = 1.0 / math.sqrt(width)
    tokens = rows * cols
    queries = feat1.reshape(tokens, width)
    init = (
        jnp.full((tokens,), -1e30, jnp.float32),
        jnp.zeros((tokens,), jnp.float32),
        jnp.zeros((tokens, width), jnp.float32),
        jnp.zeros((tokens,), jnp.float32),
        jnp.zeros((tokens,), jnp.float32),
    )

    def norm_y(index):
        return (index.astype(jnp.float32) + 0.5) * (2.0 / full_rows) - 1.0

    def norm_x(index):
        return (index.astype(jnp.float32) + 0.5) * (2.0 / full_cols) - 1.0

    piece = lax.all_gather(feat2, ("blk", "col"), axis=0, tiled=True)
    count = piece.shape[0]
    gathered = jnp.arange(count, dtype=jnp.int32)
    shard = gathered // rows
    tile_y = shard // ncol * rows + gathered % rows
    tile_x = shard % ncol * cols
    grid_y = jnp.broadcast_to(tile_y[:, None], (count, cols))
    grid_x = tile_x[:, None] + jnp.arange(cols, dtype=jnp.int32)[None, :]
    carry = absorb(
        init,
        queries,
        piece.reshape(count * cols, width),
        norm_y(grid_y).reshape(-1),
        norm_x(grid_x).reshape(-1),
        scale,
    )
    top, total, acc, along_y, along_x = carry
    warped = (acc / total[:, None]).astype(jnp.bfloat16).reshape(rows, cols, width)
    own_y = norm_y(row_start + jnp.arange(rows, dtype=jnp.int32))
    own_x = norm_x(col_start + jnp.arange(cols, dtype=jnp.int32))
    flow = jnp.stack(
        [
            (along_y / total).reshape(rows, cols) - own_y[:, None],
            (along_x / total).reshape(rows, cols) - own_x[None, :],
        ]
    )
    pair = jnp.stack([feat1, warped])
    xval = feat1.astype(jnp.float32)
    yval = warped.astype(jnp.float32)
    margin = 1
    padded = with_halo(pair, (("blk", 1), ("col", 2)), 1)
    xpad = padded[0].astype(jnp.float32)
    ypad = padded[1].astype(jnp.float32)
    first, grad_var, grad_cov = local_terms(xpad, ypad)
    maps = jnp.stack([first, grad_var, grad_cov])
    beside_all = with_halo(maps.astype(jnp.bfloat16), (("blk", 1), ("col", 2)), 1).astype(
        maps.dtype
    )
    spread_first = box_valid(beside_all[0])
    spread_var = box_valid(beside_all[1])
    spread_cov = box_valid(beside_all[2])
    grad_warped = spread_first + 2.0 * yval * spread_var + xval * spread_cov
    flow_pad = with_halo(flow, (("blk", 1), ("col", 2)), 1)
    x_rows = xpad[margin - 1 : margin + rows + 1, margin : margin + cols]
    x_cols = xpad[margin : margin + rows, margin - 1 : margin + cols + 1]
    edge_y = row_start - 1 + jnp.arange(rows + 1, dtype=jnp.int32)
    valid_y = (edge_y >= 0) & (edge_y <= full_rows - 2)
    edge_x = col_start - 1 + jnp.arange(cols + 1, dtype=jnp.int32)
    valid_x = (edge_x >= 0) & (edge_x <= full_cols - 2)
    delta_y = flow_pad[:, 1:, 1:-1] - flow_pad[:, :-1, 1:-1]
    push_y = jnp.where(
        valid_y[None, :, None],
        charbonnier(edge_weight(x_rows[:-1], x_rows[1:])[None], delta_y),
        0.0,
    )
    delta_x = flow_pad[:, 1:-1, 1:] - flow_pad[:, 1:-1, :-1]
    push_x = jnp.where(
        valid_x[None, None, :],
        charbonnier(edge_weight(x_cols[:, :-1], x_cols[:, 1:])[None], delta_x),
        0.0,
    )
    grad_flow = push_y[:, :rows] - push_y[:, 1:] + push_x[:, :, :cols] - push_x[:, :, 1:]
    return (flow, grad_flow, grad_warped)


def solution(mesh):
    placed = (P("blk", "col", None), P("blk", "col", None))
    return jax.shard_map(
        body,
        mesh=mesh,
        in_specs=placed,
        out_specs=(P(None, "blk", "col"), P(None, "blk", "col"), P("blk", "col", None)),
        check_vma=False,
    )
```

profile of v0, /device:TPU:152, one launch (start us, length us, event | category | flops | bytes accessed | tf_op | source)
XLA Modules:
  0.0 916.3 jit_solution(4387927049897352818)
XLA Ops:
  9.2 724.7 %all-gather.2.cloned.1.call-done = bf16[1024,48,256]{2,1,0:T(8,128)(2,1)} async-done(((bf16[4,48,256]{2,1,0:T(8,128)(2,1)}), bf16[1024,48,256]{2,1,0:T(8,128)(2,1)}) %all-gather.2.cloned.1.call-update) | async-done | bytes 25165840 | tf_op jit(solution)/shard_map/all_gather | solution.py:125
  734.0 100.4 %while.19 = (s32[]{:T(128)}, f32[192]{0:T(256)S(1)}, f32[192]{0:T(256)S(1)}, f32[192,256]{1,0:T(8,128)S(1)}, f32[192]{0:T(256)S(1)}, /*index=5*/f32[192]{0:T(256...) while((s32[]{:T(128)}, f32[192]{0:T(256)S(1)}, ...), condition=%wide.region_5.6_spmd.clone, body=%wide.region_0.5_spmd.clone.sunk | while | flops 406734528 | bytes 7375766 | solution.py:97
  734.0 1.8 fusion.87
  736.5 1.7 convolution_add_fusion.2
  738.2 1.8 fusion.87
  740.7 1.7 convolution_add_fusion.2
  742.3 1.8 fusion.87
  744.8 1.7 convolution_add_fusion.2
  746.5 1.8 fusion.87
  749.0 1.7 convolution_add_fusion.2
  750.7 1.8 fusion.87
  753.2 1.7 convolution_add_fusion.2
  754.9 1.8 fusion.87
  757.4 1.7 convolution_add_fusion.2
  759.1 1.8 fusion.87
  761.6 1.7 convolution_add_fusion.2
  763.3 1.8 fusion.87
  765.8 1.7 convolution_add_fusion.2
  767.4 1.8 fusion.87
  770.0 1.7 convolution_add_fusion.2
  771.6 1.8 fusion.87
  774.1 1.7 convolution_add_fusion.2
  775.8 1.8 fusion.87
  778.3 1.7 convolution_add_fusion.2
  780.0 1.8 fusion.87
  782.5 1.7 convolution_add_fusion.2
  784.2 1.8 fusion.87
  786.7 1.7 convolution_add_fusion.2
  788.4 1.8 fusion.87
  790.9 1.7 convolution_add_fusion.2
  792.6 1.8 fusion.87
  795.1 1.7 convolution_add_fusion.2
  796.7 1.8 fusion.87
  799.3 1.7 convolution_add_fusion.2
  800.9 1.8 fusion.87
  803.4 1.7 convolution_add_fusion.2
  805.1 1.8 fusion.87
  807.6 1.7 convolution_add_fusion.2
  809.3 1.8 fusion.87
  811.8 1.7 convolution_add_fusion.2
  813.5 1.8 fusion.87
  816.0 1.7 convolution_add_fusion.2
  817.7 1.8 fusion.87
  820.2 1.7 convolution_add_fusion.2
  821.9 1.8 fusion.87
  824.4 1.7 convolution_add_fusion.2
  826.0 1.8 fusion.87
  828.5 1.7 convolution_add_fusion.2
  830.2 1.8 fusion.87
  832.7 1.7 convolution_add_fusion.2
  834.7 7.1 collective-permute-start.4
  841.7 1.9 collective-permute-start.5
  844.4 5.7 collective-permute-start.1
  850.1 1.9 collective-permute-start
  852.1 5.5 collective-permute-done
  857.7 10.1 %collective-permute-start.3 = (bf16[2,6,1,256]{3,2,1,0:T(2,128)(2,1)S(1)}, bf16[2,6,1,256]{3,2,1,0:T(2,128)(2,1)S(1)}, u32[]{:S(2)}, u32[]{:S(2)}) collective-permute-start(bf16[2,6,1,256]{3,2,1,0:T(2,128)(2,1)S(1)} %get-tuple-element.148), channel_id=1, source_target_pairs={{1,0},{2,1},{3,2},{4,3},{5,4},{6,5},{7,6},{9,8},{10,9},{11,10},{12... | collective-permute-start | bytes 18440 | tf_op jit(solution)/shard_map/ppermute | solution.py:21
  867.8 12.3 %collective-permute-start.2 = (bf16[2,6,1,256]{3,2,1,0:T(2,128)(2,1)S(1)}, bf16[2,6,1,256]{3,2,1,0:T(2,128)(2,1)S(1)}, u32[]{:S(2)}, u32[]{:S(2)}) collective-permute-start(bf16[2,6,1,256]{3,2,1,0:T(2,128)(2,1)S(1)} %get-tuple-element.147), channel_id=1, source_target_pairs={{0,1},{1,2},{2,3},{3,4},{4,5},{5,6},{6,7},{8,9},{9,10},{10,11},{11... | collective-permute-start | bytes 18440 | tf_op jit(solution)/shard_map/ppermute | solution.py:20
  880.1 3.9 collective-permute-start.7
  884.1 1.9 collective-permute-start.6
  887.5 1.9 collective-permute-start.9
  889.4 2.4 collective-permute-start.8
  893.3 3.9 collective-permute-done.8
  897.3 3.2 collective-permute-start.11
  900.5 6.3 collective-permute-start.10
  (201 shorter events, 24.3 us)
Async XLA Ops:
  7.2 726.8 %copy-start = (bf16[4,48,256]{2,1,0:T(8,128)(2,1)S(1)}, bf16[4,48,256]{2,1,0:T(8,128)(2,1)}, u32[]{:S(2)}) copy-start(bf16[4,48,256]{2,1,0:T(8,128)(2,1)} %param.4) | copy-start | bytes 294916
  7.2 726.8 %all-gather.2.cloned.1.call-start = ((), (), s32[]{:S(2)}) async-start(), calls=%async_computation | async-start | bytes 25264128 | tf_op jit(solution)/shard_map/all_gather | solution.py:125
  834.7 17.4 %collective-permute-start.4 = (f32[2,1,48]{2,1,0:T(1,128)S(1)}, f32[2,1,48]{2,1,0:T(1,128)S(1)}, u32[]{:S(2)}, u32[]{:S(2)}) collective-permute-start(f32[2,1,48]{2,1,0:T(1,128)S(1)} %get-tuple-element.154), channel_id=1, source_target_pairs={{8,0},{16,8},{24,16},{32,24},{40,32},{48,40},{56,48},{64,56},{72,6... | collective-permute-start | bytes 1160 | tf_op jit(solution)/shard_map/ppermute | solution.py:21
  841.7 10.3 %collective-permute-start.5 = (f32[2,1,48]{2,1,0:T(1,128)S(1)}, f32[2,1,48]{2,1,0:T(1,128)S(1)}, u32[]{:S(2)}, u32[]{:S(2)}) collective-permute-start(f32[2,1,48]{2,1,0:T(1,128)S(1)} %get-tuple-element.153), channel_id=1, source_target_pairs={{0,8},{8,16},{16,24},{24,32},{32,40},{40,48},{48,56},{56,64},{64,7... | collective-permute-start | bytes 1160 | tf_op jit(solution)/shard_map/ppermute | solution.py:20
  844.4 7.7 collective-permute-start.1
  850.1 7.5 collective-permute-start
  857.7 28.3 %collective-permute-start.3 = (bf16[2,6,1,256]{3,2,1,0:T(2,128)(2,1)S(1)}, bf16[2,6,1,256]{3,2,1,0:T(2,128)(2,1)S(1)}, u32[]{:S(2)}, u32[]{:S(2)}) collective-permute-start(bf16[2,6,1,256]{3,2,1,0:T(2,128)(2,1)S(1)} %get-tuple-element.148), channel_id=1, source_target_pairs={{1,0},{2,1},{3,2},{4,3},{5,4},{6,5},{7,6},{9,8},{10,9},{11,10},{12... | collective-permute-start | bytes 18440 | tf_op jit(solution)/shard_map/ppermute | solution.py:21
  867.8 18.3 %collective-permute-start.2 = (bf16[2,6,1,256]{3,2,1,0:T(2,128)(2,1)S(1)}, bf16[2,6,1,256]{3,2,1,0:T(2,128)(2,1)S(1)}, u32[]{:S(2)}, u32[]{:S(2)}) collective-permute-start(bf16[2,6,1,256]{3,2,1,0:T(2,128)(2,1)S(1)} %get-tuple-element.147), channel_id=1, source_target_pairs={{0,1},{1,2},{2,3},{3,4},{4,5},{5,6},{6,7},{8,9},{9,10},{10,11},{11... | collective-permute-start | bytes 18440 | tf_op jit(solution)/shard_map/ppermute | solution.py:20
  880.1 11.8 %collective-permute-start.7 = (f32[2,6,1]{2,1,0:T(8,128)S(1)}, f32[2,6,1]{2,1,0:T(8,128)S(1)}, u32[]{:S(2)}, u32[]{:S(2)}) collective-permute-start(f32[2,6,1]{2,1,0:T(8,128)S(1)} %get-tuple-element.152), channel_id=1, source_target_pairs={{0,1},{1,2},{2,3},{3,4},{4,5},{5,6},{6,7},{8,9},{9,10},{10,11},{11... | collective-permute-start | bytes 152 | tf_op jit(solution)/shard_map/ppermute | solution.py:20
  884.1 9.2 collective-permute-start.6
  887.5 5.8 collective-permute-start.9
  889.4 7.8 collective-permute-start.8
  897.3 10.1 %collective-permute-start.11 = (bf16[3,6,1,256]{3,2,1,0:T(2,128)(2,1)S(1)}, bf16[3,6,1,256]{3,2,1,0:T(2,128)(2,1)S(1)}, u32[]{:S(2)}, u32[]{:S(2)}) collective-permute-start(bf16[3,6,1,256]{3,2,1,0:T(2,128)(2,1)S(1)} %get-tuple-element.139), channel_id=1, source_target_pairs={{1,0},{2,1},{3,2},{4,3},{5,4},{6,5},{7,6},{9,8},{10,9},{11,10},{12... | collective-permute-start | bytes 27656 | tf_op jit(solution)/shard_map/ppermute | solution.py:21
  900.5 7.7 collective-permute-start.10
Sparse Core Ops, SparseCore 0:
  9.9 724.0 all-gather.1
where the time goes:
time: 922 us; the launch traced here: 916 us
  waiting for transfers between devices  737 us (80%)
  matrix products  83.4 us (9%)
  starting transfers between devices  58.7 us (6%)
  other arithmetic  19.7 us (2%)
  between operations  14.4 us (2%)
    all_gather x1, waiting for transfers between devices, body(): piece = lax.all_gather(feat2, ('blk', 'col'), axis=0, tiled=True)  725 us
    dot_general x24, matrix products, visit(): lax.dot_general(queries, key_block, (((1,), (1,)), ((), ())), preferred_e...  43.6 us
    dot_general x24, matrix products, visit(): jnp.dot(expo.astype(jnp.bfloat16), key_block, preferred_element_type=jnp....  39.8 us
    ppermute x6, starting transfers between devices, with_halo(): after = lax.ppermute(first, axis, down)  29.9 us
    ppermute x6, starting transfers between devices, with_halo(): before = lax.ppermute(last, axis, up)  28.7 us
  transfers between devices with their start and end apart: 13, of which 5 were waited for; matrix products, arithmetic and copies ran while one was open for 0% of the time, Pallas kernels for 0%

commit v1 on v0

--- a/solution.py
+++ b/solution.py
@@ -3,11 +3,17 @@
 import jax
 import jax.numpy as jnp
 from jax import lax
+from jax.sharding import Mesh
 from jax.sharding import PartitionSpec as P
 
 ssim_one = 0.01
 ssim_two = 0.03
 charb_sq = 0.0001
+
+FINE = ("z", "xl", "c", "xh", "y")
+BLK = ("z", "xl", "c")
+COL = ("xh", "y")
+GATHER_ORDER = ("z", ("xh", "xl"), "y", "c")
 
 
 def with_halo(value, sides, width):
@@ -100,11 +106,11 @@
 
 def body(feat1, feat2):
     rows, cols, width = feat1.shape
-    ncol = lax.axis_size("col")
-    full_rows = rows * lax.axis_size("blk")
+    ncol = lax.axis_size(COL)
+    full_rows = rows * lax.axis_size(BLK)
     full_cols = cols * ncol
-    row_start = lax.axis_index("blk") * rows
-    col_start = lax.axis_index("col") * cols
+    row_start = lax.axis_index(BLK) * rows
+    col_start = lax.axis_index(COL) * cols
     scale = 1.0 / math.sqrt(width)
     tokens = rows * cols
     queries = feat1.reshape(tokens, width)
@@ -122,12 +128,23 @@
     def norm_x(index):
         return (index.astype(jnp.float32) + 0.5) * (2.0 / full_cols) - 1.0
 
-    piece = lax.all_gather(feat2, ("blk", "col"), axis=0, tiled=True)
+    piece = feat2
+    for axis in GATHER_ORDER:
+        piece = lax.all_gather(piece, axis, axis=0, tiled=True)
     count = piece.shape[0]
     gathered = jnp.arange(count, dtype=jnp.int32)
-    shard = gathered // rows
-    tile_y = shard // ncol * rows + gathered % rows
-    tile_x = shard % ncol * cols
+    rest = gathered // rows
+    place = {}
+    for axis in GATHER_ORDER:
+        size = lax.axis_size(axis)
+        place[axis] = rest % size
+        rest = rest // size
+    sz, sxl, sc, sxh, sy = (lax.axis_size(a) for a in FINE)
+    x_full = place[("xh", "xl")]
+    blk_of = (place["z"] * sxl + x_full % sxl) * sc + place["c"]
+    col_of = (x_full // sxl) * sy + place["y"]
+    tile_y = blk_of * rows + gathered % rows
+    tile_x = col_of * cols
     grid_y = jnp.broadcast_to(tile_y[:, None], (count, cols))
     grid_x = tile_x[:, None] + jnp.arange(cols, dtype=jnp.int32)[None, :]
     carry = absorb(
@@ -152,19 +169,19 @@
     xval = feat1.astype(jnp.float32)
     yval = warped.astype(jnp.float32)
     margin = 1
-    padded = with_halo(pair, (("blk", 1), ("col", 2)), 1)
+    padded = with_halo(pair, ((BLK, 1), (COL, 2)), 1)
     xpad = padded[0].astype(jnp.float32)
     ypad = padded[1].astype(jnp.float32)
     first, grad_var, grad_cov = local_terms(xpad, ypad)
     maps = jnp.stack([first, grad_var, grad_cov])
-    beside_all = with_halo(maps.astype(jnp.bfloat16), (("blk", 1), ("col", 2)), 1).astype(
+    beside_all = with_halo(maps.astype(jnp.bfloat16), ((BLK, 1), (COL, 2)), 1).astype(
         maps.dtype
     )
     spread_first = box_valid(beside_all[0])
     spread_var = box_valid(beside_all[1])
     spread_cov = box_valid(beside_all[2])
     grad_warped = spread_first + 2.0 * yval * spread_var + xval * spread_cov
-    flow_pad = with_halo(flow, (("blk", 1), ("col", 2)), 1)
+    flow_pad = with_halo(flow, ((BLK, 1), (COL, 2)), 1)
     x_rows = xpad[margin - 1 : margin + rows + 1, margin : margin + cols]
     x_cols = xpad[margin : margin + rows, margin - 1 : margin + cols + 1]
     edge_y = row_start - 1 + jnp.arange(rows + 1, dtype=jnp.int32)
@@ -188,11 +205,14 @@
 
 
 def solution(mesh):
-    placed = (P("blk", "col", None), P("blk", "col", None))
+    blk, col = mesh.devices.shape
+    fine = mesh.devices.reshape(blk // 4, 2, 2, 2, col // 2)
+    fine_mesh = Mesh(fine, FINE)
+    placed = (P(BLK, COL, None), P(BLK, COL, None))
     return jax.shard_map(
         body,
-        mesh=mesh,
+        mesh=fine_mesh,
         in_specs=placed,
-        out_specs=(P(None, "blk", "col"), P(None, "blk", "col"), P("blk", "col", None)),
+        out_specs=(P(None, BLK, COL), P(None, BLK, COL), P(BLK, COL, None)),
         check_vma=False,
     )

time: 922 us -> 419 us (0.45)
  waiting for transfers between devices: 737 us -> 224 us
  blocking collectives: 0 us -> 28.3 us
  starting transfers between devices: 58.7 us -> 42.3 us
    all_gather x1 -> x3, waiting for transfers between devices: 725 us -> 214 us  [body(): piece = lax.all_gather(piece, axis, axis=0, tiled=True)]
    all_gather x0 -> x1, blocking collectives: none -> 28.3 us  [body(): piece = lax.all_gather(piece, axis, axis=0, tiled=True)]
    ppermute x6, waiting for transfers between devices: 10.2 us -> 0.02 us  [with_halo(): before = lax.ppermute(last, axis, up)]
    ppermute x6, starting transfers between devices: 29.9 us -> 19.9 us  [with_halo(): after = lax.ppermute(first, axis, down)]
  transfers between devices with their start and end apart: 13 -> 15, of which waited for: 5 -> 6; matrix products, arithmetic and copies ran while one was open for 0% -> 1% of each run, Pallas kernels for 0% -> 0%
where the time goes in v1:
time: 419 us; the launch traced here: 415 us
  waiting for transfers between devices  224 us (53%)
  matrix products  83.6 us (20%)
  starting transfers between devices  42.3 us (10%)
  blocking collectives  28.3 us (7%)
  other arithmetic  19.7 us (5%)
  between operations  14.1 us (3%)
    all_gather x3, waiting for transfers between devices, body(): piece = lax.all_gather(piece, axis, axis=0, tiled=True)  214 us
    dot_general x24, matrix products, visit(): lax.dot_general(queries, key_block, (((1,), (1,)), ((), ())), preferred_e...  43.8 us
    dot_general x24, matrix products, visit(): jnp.dot(expo.astype(jnp.bfloat16), key_block, preferred_element_type=jnp....  39.8 us
    all_gather x1, blocking collectives, body(): piece = lax.all_gather(piece, axis, axis=0, tiled=True)  28.3 us
    ppermute x6, starting transfers between devices, with_halo(): before = lax.ppermute(last, axis, up)  22.3 us
    ppermute x6, starting transfers between devices, with_halo(): after = lax.ppermute(first, axis, down)  19.9 us
    reduce_sum x24, other arithmetic, visit(): along_x = along_x * shrink + jnp.sum(expo * block_x[None, :], axis=1)  14.2 us
    ppermute x6, waiting for transfers between devices, with_halo(): after = lax.ppermute(first, axis, down)  10.1 us
  transfers between devices with their start and end apart: 15, of which 6 were waited for; matrix products, arithmetic and copies ran while one was open for 1% of the time, Pallas kernels for 0%

profile of v1, /device:TPU:152, one launch (start us, length us, event | category | flops | bytes accessed | tf_op | source)
XLA Modules:
  0.0 414.9 jit_solution(2693076808287747564)
XLA Ops:
  7.2 28.3 %all_gather.12 = bf16[32,48,256]{2,1,0:T(8,128)(2,1)} all-gather(bf16[4,48,256]{2,1,0:T(8,128)(2,1)} %param.5), channel_id=1, replica_groups=mesh['z'=8,'xl'=2,'c'=2,'xh'=2,'y'=4] {'z'}, dimensions={0}, use_global_device_ids=true | all-gather | bytes 884736 | tf_op jit(solution)/shard_map/all_gather | solution.py:133
  35.6 43.4 %all-gather.4.cloned.1.call-done = bf16[128,48,256]{2,1,0:T(8,128)(2,1)} async-done(((bf16[32,48,256]{2,1,0:T(8,128)(2,1)}), bf16[128,48,256]{2,1,0:T(8,128)(2,1)}) %all-gather.4.cloned.1.call-update) | async-done | bytes 3145744 | tf_op jit(solution)/shard_map/all_gather | solution.py:133
  79.0 122.1 %all-gather.6.cloned.1.call-done = bf16[512,48,256]{2,1,0:T(8,128)(2,1)} async-done(((bf16[128,48,256]{2,1,0:T(8,128)(2,1)}), bf16[512,48,256]{2,1,0:T(8,128)(2,1)}) %all-gather.6.cloned.1.call-update) | async-done | bytes 12582928 | tf_op jit(solution)/shard_map/all_gather | solution.py:133
  202.5 48.1 %all-gather.8.cloned.1.call-done = bf16[1024,48,256]{2,1,0:T(8,128)(2,1)} async-done(((bf16[512,48,256]{2,1,0:T(8,128)(2,1)}), bf16[1024,48,256]{2,1,0:T(8,128)(2,1)}) %all-gather.8.cloned.1.call-update) | async-done | bytes 25165840 | tf_op jit(solution)/shard_map/all_gather | solution.py:133
  250.6 100.6 %while.19 = (s32[]{:T(128)}, f32[192]{0:T(256)S(1)}, f32[192]{0:T(256)S(1)}, f32[192,256]{1,0:T(8,128)S(1)}, f32[192]{0:T(256)S(1)}, /*index=5*/f32[192]{0:T(256...) while((s32[]{:T(128)}, f32[192]{0:T(256)S(1)}, ...), condition=%wide.region_5.6_spmd.clone, body=%wide.region_0.5_spmd.clone.sunk | while | flops 406734528 | bytes 7376774 | solution.py:103
  250.6 1.8 fusion.100
  253.0 1.7 convolution_add_fusion.2
  254.7 1.8 fusion.100
  257.2 1.7 convolution_add_fusion.2
  258.9 1.8 fusion.100
  261.4 1.7 convolution_add_fusion.2
  263.1 1.8 fusion.100
  265.6 1.7 convolution_add_fusion.2
  267.3 1.8 fusion.100
  269.8 1.7 convolution_add_fusion.2
  271.5 1.8 fusion.100
  274.0 1.7 convolution_add_fusion.2
  275.7 1.8 fusion.100
  278.2 1.7 convolution_add_fusion.2
  279.9 1.8 fusion.100
  282.4 1.7 convolution_add_fusion.2
  284.1 1.8 fusion.100
  286.6 1.7 convolution_add_fusion.2
  288.3 1.8 fusion.100
  290.8 1.7 convolution_add_fusion.2
  292.5 1.8 fusion.100
  295.0 1.7 convolution_add_fusion.2
  296.7 1.8 fusion.100
  299.2 1.7 convolution_add_fusion.2
  300.9 1.8 fusion.100
  303.4 1.7 convolution_add_fusion.2
  305.1 1.8 fusion.100
  307.6 1.7 convolution_add_fusion.2
  309.3 1.8 fusion.100
  311.7 1.7 convolution_add_fusion.2
  313.5 1.8 fusion.100
  315.9 1.7 convolution_add_fusion.2
  317.6 1.8 fusion.100
  320.1 1.7 convolution_add_fusion.2
  321.8 1.8 fusion.100
  324.3 1.7 convolution_add_fusion.2
  326.0 1.8 fusion.100
  328.5 1.7 convolution_add_fusion.2
  330.2 1.8 fusion.100
  332.7 1.7 convolution_add_fusion.2
  334.4 1.8 fusion.100
  338.6 1.8 fusion.100
  342.8 1.8 fusion.100
  347.0 1.8 fusion.100
  351.6 3.2 collective-permute-start.4
  354.7 1.9 collective-permute-start.5
  357.3 2.7 collective-permute-start
  359.9 5.0 %collective-permute-start.1 = (bf16[2,1,48,256]{3,2,1,0:T(8,128)(2,1)S(1)}, bf16[2,1,48,256]{3,2,1,0:T(8,128)(2,1)S(1)}, u32[]{:S(2)}, u32[]{:S(2)}) collective-permute-start(bf16[2,1,48,256]{3,2,1,0:T(8,128)(2,1)S(1)} %get-tuple-element.150), channel_id=1, source_target_pairs={{8,0},{16,8},{24,16},{32,24},{40,32},{48,40},{56,48},{64,56},{72,6... | collective-permute-start | bytes 147464 | tf_op jit(solution)/shard_map/ppermute | solution.py:27
  365.0 1.7 collective-permute-done.1
  366.7 4.5 %collective-permute-start.2 = (bf16[2,6,1,256]{3,2,1,0:T(2,128)(2,1)S(1)}, bf16[2,6,1,256]{3,2,1,0:T(2,128)(2,1)S(1)}, u32[]{:S(2)}, u32[]{:S(2)}) collective-permute-start(bf16[2,6,1,256]{3,2,1,0:T(2,128)(2,1)S(1)} %get-tuple-element.147), channel_id=1, source_target_pairs={{0,1},{1,2},{2,3},{3,4},{4,5},{5,6},{6,7},{8,9},{9,10},{10,11},{11... | collective-permute-start | bytes 18440 | tf_op jit(solution)/shard_map/ppermute | solution.py:26
  371.3 1.9 collective-permute-start.3
  373.3 2.1 collective-permute-start.6
  375.4 7.3 %collective-permute-start.7 = (f32[2,6,1]{2,1,0:T(8,128)S(1)}, f32[2,6,1]{2,1,0:T(8,128)S(1)}, u32[]{:S(2)}, u32[]{:S(2)}) collective-permute-start(f32[2,6,1]{2,1,0:T(8,128)S(1)} %get-tuple-element.152), channel_id=1, source_target_pairs={{0,1},{1,2},{2,3},{3,4},{4,5},{5,6},{6,7},{8,9},{9,10},{10,11},{11... | collective-permute-start | bytes 152 | tf_op jit(solution)/shard_map/ppermute | solution.py:26
  384.2 1.9 collective-permute-start.8
  386.1 5.8 %collective-permute-start.9 = (bf16[3,1,48,256]{3,2,1,0:T(8,128)(2,1)S(1)}, bf16[3,1,48,256]{3,2,1,0:T(8,128)(2,1)S(1)}, u32[]{:S(2)}, u32[]{:S(2)}) collective-permute-start(bf16[3,1,48,256]{3,2,1,0:T(8,128)(2,1)S(1)} %get-tuple-element.146), channel_id=1, source_target_pairs={{8,0},{16,8},{24,16},{32,24},{40,32},{48,40},{56,48},{64,56},{72,6... | collective-permute-start | bytes 221192 | tf_op jit(solution)/shard_map/ppermute | solution.py:27
  392.1 1.8 collective-permute-done.9
  393.9 3.9 collective-permute-start.10
  397.8 1.9 collective-permute-start.11
  400.4 6.7 %collective-permute-done.11 = bf16[3,6,1,256]{3,2,1,0:T(2,128)(2,1)S(1)} collective-permute-done((bf16[3,6,1,256]{3,2,1,0:T(2,128)(2,1)S(1)}, bf16[3,6,1,256]{3,2,1,0:T(2,128)(2,1)S(1)}, u32[]{:S(2)}, u32[]{:S(2)}) %collective-permute-start.11) | collective-permute-done | bytes 9248 | tf_op jit(solution)/shard_map/ppermute | solution.py:27
  (208 shorter events, 28.4 us)
Async XLA Ops:
  7.2 71.8 %all-gather.4.cloned.1.call-start = ((), (), s32[]{:S(2)}) async-start(), calls=%async_computation | async-start | bytes 3932160 | tf_op jit(solution)/shard_map/all_gather | solution.py:133
  35.5 165.6 %all-gather.6.cloned.1.call-start = ((), (), s32[]{:S(2)}) async-start(), calls=%async_computation.1 | async-start | bytes 15728640 | tf_op jit(solution)/shard_map/all_gather | solution.py:133
  79.0 171.6 %all-gather.8.cloned.1.call-start = ((), (), s32[]{:S(2)}) async-start(), calls=%async_computation.2 | async-start | bytes 37748736 | tf_op jit(solution)/shard_map/all_gather | solution.py:133
  201.1 49.4 %copy-start = (bf16[4,48,256]{2,1,0:T(8,128)(2,1)S(1)}, bf16[4,48,256]{2,1,0:T(8,128)(2,1)}, u32[]{:S(2)}) copy-start(bf16[4,48,256]{2,1,0:T(8,128)(2,1)} %param.4) | copy-start | bytes 294916
  351.6 13.4 %collective-permute-start.4 = (f32[2,1,48]{2,1,0:T(1,128)S(1)}, f32[2,1,48]{2,1,0:T(1,128)S(1)}, u32[]{:S(2)}, u32[]{:S(2)}) collective-permute-start(f32[2,1,48]{2,1,0:T(1,128)S(1)} %get-tuple-element.154), channel_id=1, source_target_pairs={{8,0},{16,8},{24,16},{32,24},{40,32},{48,40},{56,48},{64,56},{72,6... | collective-permute-start | bytes 1160 | tf_op jit(solution)/shard_map/ppermute | solution.py:27
  354.7 10.2 %collective-permute-start.5 = (f32[2,1,48]{2,1,0:T(1,128)S(1)}, f32[2,1,48]{2,1,0:T(1,128)S(1)}, u32[]{:S(2)}, u32[]{:S(2)}) collective-permute-start(f32[2,1,48]{2,1,0:T(1,128)S(1)} %get-tuple-element.153), channel_id=1, source_target_pairs={{0,8},{8,16},{16,24},{24,32},{32,40},{40,48},{48,56},{56,64},{64,7... | collective-permute-start | bytes 1160 | tf_op jit(solution)/shard_map/ppermute | solution.py:26
  357.3 7.7 %collective-permute-start = (bf16[2,1,48,256]{3,2,1,0:T(8,128)(2,1)S(1)}, bf16[2,1,48,256]{3,2,1,0:T(8,128)(2,1)S(1)}, u32[]{:S(2)}, u32[]{:S(2)}) collective-permute-start(bf16[2,1,48,256]{3,2,1,0:T(8,128)(2,1)S(1)} %get-tuple-element.149), channel_id=1, source_target_pairs={{0,8},{8,16},{16,24},{24,32},{32,40},{40,48},{48,56},{56,64},{64,7... | collective-permute-start | bytes 147464 | tf_op jit(solution)/shard_map/ppermute | solution.py:26
  359.9 6.7 %collective-permute-start.1 = (bf16[2,1,48,256]{3,2,1,0:T(8,128)(2,1)S(1)}, bf16[2,1,48,256]{3,2,1,0:T(8,128)(2,1)S(1)}, u32[]{:S(2)}, u32[]{:S(2)}) collective-permute-start(bf16[2,1,48,256]{3,2,1,0:T(8,128)(2,1)S(1)} %get-tuple-element.150), channel_id=1, source_target_pairs={{8,0},{16,8},{24,16},{32,24},{40,32},{48,40},{56,48},{64,56},{72,6... | collective-permute-start | bytes 147464 | tf_op jit(solution)/shard_map/ppermute | solution.py:27
  366.7 16.0 %collective-permute-start.2 = (bf16[2,6,1,256]{3,2,1,0:T(2,128)(2,1)S(1)}, bf16[2,6,1,256]{3,2,1,0:T(2,128)(2,1)S(1)}, u32[]{:S(2)}, u32[]{:S(2)}) collective-permute-start(bf16[2,6,1,256]{3,2,1,0:T(2,128)(2,1)S(1)} %get-tuple-element.147), channel_id=1, source_target_pairs={{0,1},{1,2},{2,3},{3,4},{4,5},{5,6},{6,7},{8,9},{9,10},{10,11},{11... | collective-permute-start | bytes 18440 | tf_op jit(solution)/shard_map/ppermute | solution.py:26
  371.3 11.5 %collective-permute-start.3 = (bf16[2,6,1,256]{3,2,1,0:T(2,128)(2,1)S(1)}, bf16[2,6,1,256]{3,2,1,0:T(2,128)(2,1)S(1)}, u32[]{:S(2)}, u32[]{:S(2)}) collective-permute-start(bf16[2,6,1,256]{3,2,1,0:T(2,128)(2,1)S(1)} %get-tuple-element.148), channel_id=1, source_target_pairs={{1,0},{2,1},{3,2},{4,3},{5,4},{6,5},{7,6},{9,8},{10,9},{11,10},{12... | collective-permute-start | bytes 18440 | tf_op jit(solution)/shard_map/ppermute | solution.py:27
  373.3 18.7 %collective-permute-start.6 = (f32[2,6,1]{2,1,0:T(8,128)S(1)}, f32[2,6,1]{2,1,0:T(8,128)S(1)}, u32[]{:S(2)}, u32[]{:S(2)}) collective-permute-start(f32[2,6,1]{2,1,0:T(8,128)S(1)} %get-tuple-element.151), channel_id=1, source_target_pairs={{1,0},{2,1},{3,2},{4,3},{5,4},{6,5},{7,6},{9,8},{10,9},{11,10},{12... | collective-permute-start | bytes 152 | tf_op jit(solution)/shard_map/ppermute | solution.py:27
  375.4 16.6 %collective-permute-start.7 = (f32[2,6,1]{2,1,0:T(8,128)S(1)}, f32[2,6,1]{2,1,0:T(8,128)S(1)}, u32[]{:S(2)}, u32[]{:S(2)}) collective-permute-start(f32[2,6,1]{2,1,0:T(8,128)S(1)} %get-tuple-element.152), channel_id=1, source_target_pairs={{0,1},{1,2},{2,3},{3,4},{4,5},{5,6},{6,7},{8,9},{9,10},{10,11},{11... | collective-permute-start | bytes 152 | tf_op jit(solution)/shard_map/ppermute | solution.py:26
  384.2 7.9 %collective-permute-start.8 = (bf16[3,1,48,256]{3,2,1,0:T(8,128)(2,1)S(1)}, bf16[3,1,48,256]{3,2,1,0:T(8,128)(2,1)S(1)}, u32[]{:S(2)}, u32[]{:S(2)}) collective-permute-start(bf16[3,1,48,256]{3,2,1,0:T(8,128)(2,1)S(1)} %get-tuple-element.145), channel_id=1, source_target_pairs={{0,8},{8,16},{16,24},{24,32},{32,40},{40,48},{48,56},{56,64},{64,7... | collective-permute-start | bytes 221192 | tf_op jit(solution)/shard_map/ppermute | solution.py:26
  386.1 7.7 %collective-permute-start.9 = (bf16[3,1,48,256]{3,2,1,0:T(8,128)(2,1)S(1)}, bf16[3,1,48,256]{3,2,1,0:T(8,128)(2,1)S(1)}, u32[]{:S(2)}, u32[]{:S(2)}) collective-permute-start(bf16[3,1,48,256]{3,2,1,0:T(8,128)(2,1)S(1)} %get-tuple-element.146), channel_id=1, source_target_pairs={{8,0},{16,8},{24,16},{32,24},{40,32},{48,40},{56,48},{64,56},{72,6... | collective-permute-start | bytes 221192 | tf_op jit(solution)/shard_map/ppermute | solution.py:27
  393.9 6.5 %collective-permute-start.10 = (bf16[3,6,1,256]{3,2,1,0:T(2,128)(2,1)S(1)}, bf16[3,6,1,256]{3,2,1,0:T(2,128)(2,1)S(1)}, u32[]{:S(2)}, u32[]{:S(2)}) collective-permute-start(bf16[3,6,1,256]{3,2,1,0:T(2,128)(2,1)S(1)} %get-tuple-element.138), channel_id=1, source_target_pairs={{0,1},{1,2},{2,3},{3,4},{4,5},{5,6},{6,7},{8,9},{9,10},{10,11},{11... | collective-permute-start | bytes 27656 | tf_op jit(solution)/shard_map/ppermute | solution.py:26
  397.8 9.3 %collective-permute-start.11 = (bf16[3,6,1,256]{3,2,1,0:T(2,128)(2,1)S(1)}, bf16[3,6,1,256]{3,2,1,0:T(2,128)(2,1)S(1)}, u32[]{:S(2)}, u32[]{:S(2)}) collective-permute-start(bf16[3,6,1,256]{3,2,1,0:T(2,128)(2,1)S(1)} %get-tuple-element.139), channel_id=1, source_target_pairs={{1,0},{2,1},{3,2},{4,3},{5,4},{6,5},{7,6},{9,8},{10,9},{11,10},{12... | collective-permute-start | bytes 27656 | tf_op jit(solution)/shard_map/ppermute | solution.py:27
Sparse Core Ops, SparseCore 0:
  35.6 43.2 all-gather.3
  80.7 120.3 all-gather.5
  202.9 47.6 all-gather.7

commit v2 on v1

--- a/solution.py
+++ b/solution.py
@@ -13,7 +13,8 @@
 FINE = ("z", "xl", "c", "xh", "y")
 BLK = ("z", "xl", "c")
 COL = ("xh", "y")
-GATHER_ORDER = ("z", ("xh", "xl"), "y", "c")
+KEY_AXES = ("z", ("xh", "xl"))
+QUERY_AXES = ("y", "c")
 
 
 def with_halo(value, sides, width):
@@ -113,13 +114,14 @@
     col_start = lax.axis_index(COL) * cols
     scale = 1.0 / math.sqrt(width)
     tokens = rows * cols
-    queries = feat1.reshape(tokens, width)
+    queries = lax.all_gather(feat1.reshape(tokens, width), QUERY_AXES, axis=0, tiled=True)
+    group = queries.shape[0]
     init = (
-        jnp.full((tokens,), -1e30, jnp.float32),
-        jnp.zeros((tokens,), jnp.float32),
-        jnp.zeros((tokens, width), jnp.float32),
-        jnp.zeros((tokens,), jnp.float32),
-        jnp.zeros((tokens,), jnp.float32),
+        jnp.full((group,), -1e30, jnp.float32),
+        jnp.zeros((group,), jnp.float32),
+        jnp.zeros((group, width), jnp.float32),
+        jnp.zeros((group,), jnp.float32),
+        jnp.zeros((group,), jnp.float32),
     )
 
     def norm_y(index):
@@ -129,20 +131,20 @@
         return (index.astype(jnp.float32) + 0.5) * (2.0 / full_cols) - 1.0
 
     piece = feat2
-    for axis in GATHER_ORDER:
+    for axis in KEY_AXES:
         piece = lax.all_gather(piece, axis, axis=0, tiled=True)
     count = piece.shape[0]
     gathered = jnp.arange(count, dtype=jnp.int32)
     rest = gathered // rows
     place = {}
-    for axis in GATHER_ORDER:
+    for axis in KEY_AXES:
         size = lax.axis_size(axis)
         place[axis] = rest % size
         rest = rest // size
     sz, sxl, sc, sxh, sy = (lax.axis_size(a) for a in FINE)
     x_full = place[("xh", "xl")]
-    blk_of = (place["z"] * sxl + x_full % sxl) * sc + place["c"]
-    col_of = (x_full // sxl) * sy + place["y"]
+    blk_of = (place["z"] * sxl + x_full % sxl) * sc + lax.axis_index("c")
+    col_of = (x_full // sxl) * sy + lax.axis_index("y")
     tile_y = blk_of * rows + gathered % rows
     tile_x = col_of * cols
     grid_y = jnp.broadcast_to(tile_y[:, None], (count, cols))
@@ -156,6 +158,12 @@
         scale,
     )
     top, total, acc, along_y, along_x = carry
+    peak = lax.pmax(top, QUERY_AXES)
+    factor = jnp.exp(top - peak)
+    acc = lax.psum_scatter(acc * factor[:, None], QUERY_AXES, scatter_dimension=0, tiled=True)
+    stats = jnp.stack([total * factor, along_y * factor, along_x * factor])
+    stats = lax.psum_scatter(stats, QUERY_AXES, scatter_dimension=1, tiled=True)
+    total, along_y, along_x = stats[0], stats[1], stats[2]
     warped = (acc / total[:, None]).astype(jnp.bfloat16).reshape(rows, cols, width)
     own_y = norm_y(row_start + jnp.arange(rows, dtype=jnp.int32))
     own_x = norm_x(col_start + jnp.arange(cols, dtype=jnp.int32))

time: 419 us -> 283 us (0.68)
  waiting for transfers between devices: 224 us -> 101 us
  matrix products: 83.6 us -> 34.6 us
  blocking collectives: 28.3 us -> 52.7 us
  other arithmetic: 19.7 us -> 32.3 us
    all_gather x3 -> x1, waiting for transfers between devices: 214 us -> 29.2 us  [body(): piece = lax.all_gather(piece, axis, axis=0, tiled=True)]
    unnamed x3 -> x4, waiting for transfers between devices: 0.05 us -> 31.6 us
    reduce_scatter x0 -> x1, waiting for transfers between devices: none -> 28.6 us  [body(): lax.psum_scatter(acc * factor[:, None], QUERY_AXES, scatter_dimension=0,...]
    dot_general x24 -> x3, matrix products: 39.8 us -> 11.8 us  [visit(): jnp.dot(expo.astype(jnp.bfloat16), key_block, preferred_element_type=jnp....]
    dot_general x24 -> x3, matrix products: 43.8 us -> 22.8 us  [visit(): lax.dot_general(queries, key_block, (((1,), (1,)), ((), ())), preferred_e...]
    all_gather x0 -> x1, blocking collectives: none -> 13.6 us  [body(): lax.all_gather(feat1.reshape(tokens, width), QUERY_AXES, axis=0, tiled=True)]
    ppermute x6, waiting for transfers between devices: 0.02 us -> 11.5 us  [with_halo(): before = lax.ppermute(last, axis, up)]
    reduce_sum x24 -> x3, other arithmetic: 14.2 us -> 25.3 us  [visit(): along_x = along_x * shrink + jnp.sum(expo * block_x[None, :], axis=1)]
  transfers between devices with their start and end apart: 15 -> 15, of which waited for: 6 -> 6; matrix products, arithmetic and copies ran while one was open for 1% -> 3% of each run, Pallas kernels for 0% -> 0%
where the time goes in v2:
time: 283 us; the launch traced here: 279 us
  waiting for transfers between devices  101 us (36%)
  blocking collectives  52.7 us (19%)
  starting transfers between devices  41.2 us (15%)
  matrix products  34.6 us (12%)
  other arithmetic  32.3 us (11%)
  between operations  14.2 us (5%)
  local copies, waits for them, and re-layouts  3.28 us (1%)
    unnamed x4, waiting for transfers between devices  31.6 us
    all_gather x1, waiting for transfers between devices, body(): piece = lax.all_gather(piece, axis, axis=0, tiled=True)  29.2 us
    reduce_scatter x1, waiting for transfers between devices, body(): lax.psum_scatter(acc * factor[:, None], QUERY_AXES, scatter_dimension=0,...  28.6 us
    all_gather x1, blocking collectives, body(): piece = lax.all_gather(piece, axis, axis=0, tiled=True)  28.3 us
    reduce_sum x3, other arithmetic, visit(): along_x = along_x * shrink + jnp.sum(expo * block_x[None, :], axis=1)  25.3 us
    ppermute x6, starting transfers between devices, with_halo(): before = lax.ppermute(last, axis, up)  23.4 us
    dot_general x3, matrix products, visit(): lax.dot_general(queries, key_block, (((1,), (1,)), ((), ())), preferred_e...  22.8 us
    ppermute x6, starting transfers between devices, with_halo(): after = lax.ppermute(first, axis, down)  17.7 us
  transfers between devices with their start and end apart: 15, of which 6 were waited for; matrix products, arithmetic and copies ran while one was open for 3% of the time, Pallas kernels for 0%

profile of v2, /device:TPU:152, one launch (start us, length us, event | category | flops | bytes accessed | tf_op | source)
XLA Modules:
  0.0 279.4 jit_solution(13142789420334072183)
XLA Ops:
  7.2 0.0 all-gather.2.cloned.1.call-start
  7.2 28.3 %all_gather.9 = bf16[32,48,256]{2,1,0:T(8,128)(2,1)} all-gather(bf16[4,48,256]{2,1,0:T(8,128)(2,1)} %param.5), channel_id=1, replica_groups=mesh['z'=8,'xl'=2,'c'=2,'xh'=2,'y'=4] {'z'}, dimensions={0}, use_global_device_ids=true | all-gather | bytes 884736 | tf_op jit(solution)/shard_map/all_gather | solution.py:135
  35.5 0.0 all-gather.2.cloned.1.call-update
  35.5 0.0 reduce-scatter.7.cloned.1.call-start
  35.7 0.1 broadcast_in_dim.34
  35.7 0.1 sub.120
  35.9 0.1 multiply_add_fusion.2
  36.0 0.1 reshape.260
  36.1 13.6 %all_gather.11 = bf16[1536,256]{1,0:T(8,128)(2,1)S(1)} all-gather(bf16[192,256]{1,0:T(8,128)(2,1)} %bitcast.60), channel_id=1, replica_groups=mesh['z'=8,'xl'=2,'c'=2,'xh'=2,'y'=4] {'y','c'}, dimensions={0}, use_global_device_ids=true | all-gather | bytes 884736 | tf_op jit(solution)/shard_map/all_gather | solution.py:117
  49.7 29.2 %all-gather.2.cloned.1.call-done = bf16[128,48,256]{2,1,0:T(8,128)(2,1)} async-done(((bf16[32,48,256]{2,1,0:T(8,128)(2,1)}), bf16[128,48,256]{2,1,0:T(8,128)(2,1)}) %all-gather.2.cloned.1.call-update) | async-done | bytes 3145744 | tf_op jit(solution)/shard_map/all_gather | solution.py:135
  78.9 60.3 %while.19 = (s32[]{:T(128)}, f32[1536]{0:T(1024)S(1)}, f32[1536]{0:T(1024)S(1)}, f32[1536,256]{1,0:T(8,128)S(1)}, f32[1536]{0:T(1024)S(1)}, /*index=5*/f32[1536]...) while((s32[]{:T(128)}, f32[1536]{0:T(1024)S(1)}, ...), condition=%wide.region_5.6_spmd.clone, body=%wide.region_0.5_spmd.clone.sunk | while | flops 3260167680 | bytes 94312616 | solution.py:104
  79.0 7.6 %multiply_reduce_fusion.5 = (f32[1536]{0:T(1024)S(1)}, f32[2048,1536]{1,0:T(8,128)}) fusion(bf16[1536,256]{1,0:T(8,128)(2,1)S(1)} %get-tuple-element.282, bf16[3,2048,256]{2,1,0:T(8,128)(2,1)} %get-tuple-element.281, s32[]{:T(128)S(6)} %copy.16), kind=kOutput, calls=%fused_computation.3.clone.1 | convolution fusion | flops 1616902656 | bytes 14424068 | tf_op jit(solution)/shard_map/while/body/eval_jaxpr/dot_general | solution.py:83
  86.5 8.4 %multiply_reduce_fusion.6 = (f32[1536]{0:T(1024)S(1)}, f32[1536]{0:T(1024)S(1)}, f32[1536]{0:T(1024)S(1)}) fusion(f32[2048]{0:T(1024)S(1)} %bitcast.68, f32[1536]{0:T(1024)S(1)} %select_maximum_fusion.2, f32[2048,1536]{1,0:T(8,128)} %get-tuple-element.242, f32[2048]{0:T(1024)S(1)} %bitcast.69), kind=kLoop, calls=%fused_computation.clone.1 | loop fusion | flops 22015488 | bytes 12623872 | tf_op jit(solution)/shard_map/while/body/eval_jaxpr/reduce_sum | solution.py:96
  95.0 3.9 %fusion.81 = f32[1536,256]{1,0:T(8,128)S(1)} fusion(f32[1536]{0:T(1024)S(1)} %select_maximum_fusion.2, f32[2048,1536]{1,0:T(8,128)S(1)} %copy-done, f32[1536,256]{1,0:T(8,128)S(1)} %get-tuple-element.266, bf16[3,2048,256]{2,1,0:T(8,128)(2,1)} %get-tuple-element.281, s32[]{:T(128)S(6)} %copy.16, f32[1536]{0:T(1024)S(1)} %get-tuple-element.246, ...), kind=kOutput, calls=%fused_computation.7.clone.1 | convolution fusion | flops 1621229568 | bytes 16789508 | tf_op jit(solution)/shard_map/while/body/eval_jaxpr/dot_general | solution.py:92
  99.0 7.6 %multiply_reduce_fusion.5 = (f32[1536]{0:T(1024)S(1)}, f32[2048,1536]{1,0:T(8,128)}) fusion(bf16[1536,256]{1,0:T(8,128)(2,1)S(1)} %get-tuple-element.282, bf16[3,2048,256]{2,1,0:T(8,128)(2,1)} %get-tuple-element.281, s32[]{:T(128)S(6)} %copy.16), kind=kOutput, calls=%fused_computation.3.clone.1 | convolution fusion | flops 1616902656 | bytes 14424068 | tf_op jit(solution)/shard_map/while/body/eval_jaxpr/dot_general | solution.py:83
  106.6 8.4 %multiply_reduce_fusion.6 = (f32[1536]{0:T(1024)S(1)}, f32[1536]{0:T(1024)S(1)}, f32[1536]{0:T(1024)S(1)}) fusion(f32[2048]{0:T(1024)S(1)} %bitcast.68, f32[1536]{0:T(1024)S(1)} %select_maximum_fusion.2, f32[2048,1536]{1,0:T(8,128)} %get-tuple-element.242, f32[2048]{0:T(1024)S(1)} %bitcast.69), kind=kLoop, calls=%fused_computation.clone.1 | loop fusion | flops 22015488 | bytes 12623872 | tf_op jit(solution)/shard_map/while/body/eval_jaxpr/reduce_sum | solution.py:96
  115.1 3.9 %fusion.81 = f32[1536,256]{1,0:T(8,128)S(1)} fusion(f32[1536]{0:T(1024)S(1)} %select_maximum_fusion.2, f32[2048,1536]{1,0:T(8,128)S(1)} %copy-done, f32[1536,256]{1,0:T(8,128)S(1)} %get-tuple-element.266, bf16[3,2048,256]{2,1,0:T(8,128)(2,1)} %get-tuple-element.281, s32[]{:T(128)S(6)} %copy.16, f32[1536]{0:T(1024)S(1)} %get-tuple-element.246, ...), kind=kOutput, calls=%fused_computation.7.clone.1 | convolution fusion | flops 1621229568 | bytes 16789508 | tf_op jit(solution)/shard_map/while/body/eval_jaxpr/dot_general | solution.py:92
  119.1 7.6 %multiply_reduce_fusion.5 = (f32[1536]{0:T(1024)S(1)}, f32[2048,1536]{1,0:T(8,128)}) fusion(bf16[1536,256]{1,0:T(8,128)(2,1)S(1)} %get-tuple-element.282, bf16[3,2048,256]{2,1,0:T(8,128)(2,1)} %get-tuple-element.281, s32[]{:T(128)S(6)} %copy.16), kind=kOutput, calls=%fused_computation.3.clone.1 | convolution fusion | flops 1616902656 | bytes 14424068 | tf_op jit(solution)/shard_map/while/body/eval_jaxpr/dot_general | solution.py:83
  126.7 8.4 %multiply_reduce_fusion.6 = (f32[1536]{0:T(1024)S(1)}, f32[1536]{0:T(1024)S(1)}, f32[1536]{0:T(1024)S(1)}) fusion(f32[2048]{0:T(1024)S(1)} %bitcast.68, f32[1536]{0:T(1024)S(1)} %select_maximum_fusion.2, f32[2048,1536]{1,0:T(8,128)} %get-tuple-element.242, f32[2048]{0:T(1024)S(1)} %bitcast.69), kind=kLoop, calls=%fused_computation.clone.1 | loop fusion | flops 22015488 | bytes 12623872 | tf_op jit(solution)/shard_map/while/body/eval_jaxpr/reduce_sum | solution.py:96
  135.2 3.9 %fusion.81 = f32[1536,256]{1,0:T(8,128)S(1)} fusion(f32[1536]{0:T(1024)S(1)} %select_maximum_fusion.2, f32[2048,1536]{1,0:T(8,128)S(1)} %copy-done, f32[1536,256]{1,0:T(8,128)S(1)} %get-tuple-element.266, bf16[3,2048,256]{2,1,0:T(8,128)(2,1)} %get-tuple-element.281, s32[]{:T(128)S(6)} %copy.16, f32[1536]{0:T(1024)S(1)} %get-tuple-element.246, ...), kind=kOutput, calls=%fused_computation.7.clone.1 | convolution fusion | flops 1621229568 | bytes 16789508 | tf_op jit(solution)/shard_map/while/body/eval_jaxpr/dot_general | solution.py:92
  139.2 10.8 %pmax.7 = f32[1536]{0:T(1024)S(1)} all-reduce(f32[1536]{0:T(1024)S(1)} %get-tuple-element.60), channel_id=1, replica_groups=mesh['z'=8,'xl'=2,'c'=2,'xh'=2,'y'=4] {'y','c'}, use_global_device_ids=true, to_apply=%region_6.7 | all-reduce | flops 1536 | bytes 12288 | tf_op jit(solution)/shard_map/pmax | solution.py:161
  150.1 1.2 copy.5
  151.3 0.0 reduce-scatter.5.cloned.1.call-start
  151.3 1.4 broadcast_multiply_fusion
  152.9 31.5 %reduce-scatter.7.cloned.1.call-done = f32[192,3]{1,0:T(8,128)} async-done(((f32[1536,3]{1,0:T(8,128)}), f32[192,3]{1,0:T(8,128)}) %reduce-scatter.7.cloned.1.call-update) | async-done | bytes 2320
  184.4 1.1 fusion.66
  185.5 0.1 copy.7
  185.6 0.1 copy.8
  185.7 0.1 copy.9
  185.8 0.1 div.129
  185.9 0.1 div.127
  186.0 0.1 broadcast_subtract_fusion
  186.1 4.0 %collective-permute-start.4 = (f32[2,1,48]{2,1,0:T(1,128)S(1)}, f32[2,1,48]{2,1,0:T(1,128)S(1)}, u32[]{:S(2)}, u32[]{:S(2)}) collective-permute-start(f32[2,1,48]{2,1,0:T(1,128)S(1)} %get-tuple-element.165), channel_id=1, source_target_pairs={{8,0},{16,8},{24,16},{32,24},{40,32},{48,40},{56,48},{64,56},{72,6... | collective-permute-start | bytes 1160 | tf_op jit(solution)/shard_map/ppermute | solution.py:28
  190.1 1.9 collective-permute-start.5
  192.0 0.6 pad_maximum_fusion.17
  192.6 28.6 %reduce-scatter.5.cloned.1.call-done = f32[192,256]{1,0:T(8,128)} async-done(((f32[1536,256]{1,0:T(8,128)}), f32[192,256]{1,0:T(8,128)}) %reduce-scatter.5.cloned.1.call-update) | async-done | bytes 196624 | tf_op jit(solution)/shard_map/reduce_scatter | solution.py:163
  221.2 1.0 convert_multiply_fusion
  222.3 4.2 %collective-permute-start.1 = (bf16[2,1,48,256]{3,2,1,0:T(8,128)(2,1)S(1)}, bf16[2,1,48,256]{3,2,1,0:T(8,128)(2,1)S(1)}, u32[]{:S(2)}, u32[]{:S(2)}) collective-permute-start(bf16[2,1,48,256]{3,2,1,0:T(8,128)(2,1)S(1)} %get-tuple-element.156), channel_id=1, source_target_pairs={{8,0},{16,8},{24,16},{32,24},{40,32},{48,40},{56,48},{64,56},{72,6... | collective-permute-start | bytes 147464 | tf_op jit(solution)/shard_map/ppermute | solution.py:28
  226.5 1.9 collective-permute-start
  228.4 5.5 %collective-permute-done = bf16[2,1,48,256]{3,2,1,0:T(8,128)(2,1)S(1)} collective-permute-done((bf16[2,1,48,256]{3,2,1,0:T(8,128)(2,1)S(1)}, bf16[2,1,48,256]{3,2,1,0:T(8,128)(2,1)S(1)}, u32[]{:S(2)}, u32[]{:S(2)}) %collective-permute-start) | collective-permute-done | bytes 49184 | tf_op jit(solution)/shard_map/ppermute | solution.py:27
  234.0 1.9 collective-permute-start.3
  235.9 7.5 %collective-permute-start.2 = (bf16[2,6,1,256]{3,2,1,0:T(2,128)(2,1)S(1)}, bf16[2,6,1,256]{3,2,1,0:T(2,128)(2,1)S(1)}, u32[]{:S(2)}, u32[]{:S(2)}) collective-permute-start(bf16[2,6,1,256]{3,2,1,0:T(2,128)(2,1)S(1)} %get-tuple-element.153), channel_id=1, source_target_pairs={{0,1},{1,2},{2,3},{3,4},{4,5},{5,6},{6,7},{8,9},{9,10},{10,11},{11... | collective-permute-start | bytes 18440 | tf_op jit(solution)/shard_map/ppermute | solution.py:27
  243.5 0.1 fusion.67
  243.6 2.1 collective-permute-start.7
  245.7 3.7 %collective-permute-start.6 = (f32[2,6,1]{2,1,0:T(8,128)S(1)}, f32[2,6,1]{2,1,0:T(8,128)S(1)}, u32[]{:S(2)}, u32[]{:S(2)}) collective-permute-start(f32[2,6,1]{2,1,0:T(8,128)S(1)} %get-tuple-element.160), channel_id=1, source_target_pairs={{1,0},{2,1},{3,2},{4,3},{5,4},{6,5},{7,6},{9,8},{10,9},{11,10},{12... | collective-permute-start | bytes 152 | tf_op jit(solution)/shard_map/ppermute | solution.py:28
  249.4 0.1 pad_maximum_fusion
  249.5 0.1 fusion.43
  249.6 0.1 fusion.20
  249.7 0.1 fusion.18
  249.8 0.1 fusion.46
  250.0 0.8 fusion.50
  250.7 0.1 convert_bitcast_fusion
  250.9 1.9 collective-permute-start.9
  252.9 2.4 collective-permute-start.8
  255.3 0.1 multiply_select_fusion
  255.3 0.1 multiply_select_fusion.1
  255.4 5.2 %collective-permute-done.8 = bf16[3,1,48,256]{3,2,1,0:T(8,128)(2,1)S(1)} collective-permute-done((bf16[3,1,48,256]{3,2,1,0:T(8,128)(2,1)S(1)}, bf16[3,1,48,256]{3,2,1,0:T(8,128)(2,1)S(1)}, u32[]{:S(2)}, u32[]{:S(2)}) %collective-permute-start.8) | collective-permute-done | bytes 73760 | tf_op jit(solution)/shard_map/ppermute | solution.py:27
  260.7 1.9 collective-permute-start.11
  262.6 7.5 %collective-permute-start.10 = (bf16[3,6,1,256]{3,2,1,0:T(2,128)(2,1)S(1)}, bf16[3,6,1,256]{3,2,1,0:T(2,128)(2,1)S(1)}, u32[]{:S(2)}, u32[]{:S(2)}) collective-permute-start(bf16[3,6,1,256]{3,2,1,0:T(2,128)(2,1)S(1)} %get-tuple-element.144), channel_id=1, source_target_pairs={{0,1},{1,2},{2,3},{3,4},{4,5},{5,6},{6,7},{8,9},{9,10},{10,11},{11... | collective-permute-start | bytes 27656 | tf_op jit(solution)/shard_map/ppermute | solution.py:27
  270.1 0.7 slice_subtract_fusion.2
  270.8 0.8 collective-permute-done.10
  271.6 0.1 maximum_convert_fusion
  271.7 0.1 slice_bitcast_fusion.2
  271.8 1.0 fusion.23
  (60 shorter events, 0.5 us)
Async XLA Ops:
  7.2 71.8 %all-gather.2.cloned.1.call-start = ((), (), s32[]{:S(2)}) async-start(), calls=%async_computation.2 | async-start | bytes 3932160 | tf_op jit(solution)/shard_map/all_gather | solution.py:135
  35.5 148.8 %reduce-scatter.7.cloned.1.call-start = ((), (), s32[]{:S(2)}) async-start(), calls=%async_computation.4 | async-start | bytes 884736
  86.5 8.5 %copy-start = (f32[2048,1536]{1,0:T(8,128)S(1)}, f32[2048,1536]{1,0:T(8,128)}, u32[]{:S(2)}) copy-start(f32[2048,1536]{1,0:T(8,128)} %get-tuple-element.242) | copy-start | bytes 37748740 | tf_op jit(solution)/shard_map/while
  106.6 8.5 %copy-start = (f32[2048,1536]{1,0:T(8,128)S(1)}, f32[2048,1536]{1,0:T(8,128)}, u32[]{:S(2)}) copy-start(f32[2048,1536]{1,0:T(8,128)} %get-tuple-element.242) | copy-start | bytes 37748740 | tf_op jit(solution)/shard_map/while
  126.7 8.5 %copy-start = (f32[2048,1536]{1,0:T(8,128)S(1)}, f32[2048,1536]{1,0:T(8,128)}, u32[]{:S(2)}) copy-start(f32[2048,1536]{1,0:T(8,128)} %get-tuple-element.242) | copy-start | bytes 37748740 | tf_op jit(solution)/shard_map/while
  139.2 83.1 %copy-start.1 = (bf16[4,48,256]{2,1,0:T(8,128)(2,1)S(1)}, bf16[4,48,256]{2,1,0:T(8,128)(2,1)}, u32[]{:S(2)}) copy-start(bf16[4,48,256]{2,1,0:T(8,128)(2,1)} %param.4) | copy-start | bytes 294916
  151.3 70.0 %reduce-scatter.5.cloned.1.call-start = ((), (), s32[]{:S(2)}) async-start(), calls=%async_computation.3 | async-start | bytes 1769472 | tf_op jit(solution)/shard_map/reduce_scatter | solution.py:163
  186.1 42.3 %collective-permute-start.4 = (f32[2,1,48]{2,1,0:T(1,128)S(1)}, f32[2,1,48]{2,1,0:T(1,128)S(1)}, u32[]{:S(2)}, u32[]{:S(2)}) collective-permute-start(f32[2,1,48]{2,1,0:T(1,128)S(1)} %get-tuple-element.165), channel_id=1, source_target_pairs={{8,0},{16,8},{24,16},{32,24},{40,32},{48,40},{56,48},{64,56},{72,6... | collective-permute-start | bytes 1160 | tf_op jit(solution)/shard_map/ppermute | solution.py:28
  190.1 38.3 %collective-permute-start.5 = (f32[2,1,48]{2,1,0:T(1,128)S(1)}, f32[2,1,48]{2,1,0:T(1,128)S(1)}, u32[]{:S(2)}, u32[]{:S(2)}) collective-permute-start(f32[2,1,48]{2,1,0:T(1,128)S(1)} %get-tuple-element.164), channel_id=1, source_target_pairs={{0,8},{8,16},{16,24},{24,32},{32,40},{40,48},{48,56},{56,64},{64,7... | collective-permute-start | bytes 1160 | tf_op jit(solution)/shard_map/ppermute | solution.py:27
  222.3 6.1 %collective-permute-start.1 = (bf16[2,1,48,256]{3,2,1,0:T(8,128)(2,1)S(1)}, bf16[2,1,48,256]{3,2,1,0:T(8,128)(2,1)S(1)}, u32[]{:S(2)}, u32[]{:S(2)}) collective-permute-start(bf16[2,1,48,256]{3,2,1,0:T(8,128)(2,1)S(1)} %get-tuple-element.156), channel_id=1, source_target_pairs={{8,0},{16,8},{24,16},{32,24},{40,32},{48,40},{56,48},{64,56},{72,6... | collective-permute-start | bytes 147464 | tf_op jit(solution)/shard_map/ppermute | solution.py:28
  226.5 7.5 %collective-permute-start = (bf16[2,1,48,256]{3,2,1,0:T(8,128)(2,1)S(1)}, bf16[2,1,48,256]{3,2,1,0:T(8,128)(2,1)S(1)}, u32[]{:S(2)}, u32[]{:S(2)}) collective-permute-start(bf16[2,1,48,256]{3,2,1,0:T(8,128)(2,1)S(1)} %get-tuple-element.155), channel_id=1, source_target_pairs={{0,8},{8,16},{16,24},{24,32},{32,40},{40,48},{48,56},{56,64},{64,7... | collective-permute-start | bytes 147464 | tf_op jit(solution)/shard_map/ppermute | solution.py:27
  234.0 15.4 %collective-permute-start.3 = (bf16[2,6,1,256]{3,2,1,0:T(2,128)(2,1)S(1)}, bf16[2,6,1,256]{3,2,1,0:T(2,128)(2,1)S(1)}, u32[]{:S(2)}, u32[]{:S(2)}) collective-permute-start(bf16[2,6,1,256]{3,2,1,0:T(2,128)(2,1)S(1)} %get-tuple-element.154), channel_id=1, source_target_pairs={{1,0},{2,1},{3,2},{4,3},{5,4},{6,5},{7,6},{9,8},{10,9},{11,10},{12... | collective-permute-start | bytes 18440 | tf_op jit(solution)/shard_map/ppermute | solution.py:28
  235.9 13.5 %collective-permute-start.2 = (bf16[2,6,1,256]{3,2,1,0:T(2,128)(2,1)S(1)}, bf16[2,6,1,256]{3,2,1,0:T(2,128)(2,1)S(1)}, u32[]{:S(2)}, u32[]{:S(2)}) collective-permute-start(bf16[2,6,1,256]{3,2,1,0:T(2,128)(2,1)S(1)} %get-tuple-element.153), channel_id=1, source_target_pairs={{0,1},{1,2},{2,3},{3,4},{4,5},{5,6},{6,7},{8,9},{9,10},{10,11},{11... | collective-permute-start | bytes 18440 | tf_op jit(solution)/shard_map/ppermute | solution.py:27
  243.6 11.8 %collective-permute-start.7 = (f32[2,6,1]{2,1,0:T(8,128)S(1)}, f32[2,6,1]{2,1,0:T(8,128)S(1)}, u32[]{:S(2)}, u32[]{:S(2)}) collective-permute-start(f32[2,6,1]{2,1,0:T(8,128)S(1)} %get-tuple-element.161), channel_id=1, source_target_pairs={{0,1},{1,2},{2,3},{3,4},{4,5},{5,6},{6,7},{8,9},{9,10},{10,11},{11... | collective-permute-start | bytes 152 | tf_op jit(solution)/shard_map/ppermute | solution.py:27
  245.7 9.7 %collective-permute-start.6 = (f32[2,6,1]{2,1,0:T(8,128)S(1)}, f32[2,6,1]{2,1,0:T(8,128)S(1)}, u32[]{:S(2)}, u32[]{:S(2)}) collective-permute-start(f32[2,6,1]{2,1,0:T(8,128)S(1)} %get-tuple-element.160), channel_id=1, source_target_pairs={{1,0},{2,1},{3,2},{4,3},{5,4},{6,5},{7,6},{9,8},{10,9},{11,10},{12... | collective-permute-start | bytes 152 | tf_op jit(solution)/shard_map/ppermute | solution.py:28
  250.9 4.5 %collective-permute-start.9 = (bf16[3,1,48,256]{3,2,1,0:T(8,128)(2,1)S(1)}, bf16[3,1,48,256]{3,2,1,0:T(8,128)(2,1)S(1)}, u32[]{:S(2)}, u32[]{:S(2)}) collective-permute-start(bf16[3,1,48,256]{3,2,1,0:T(8,128)(2,1)S(1)} %get-tuple-element.152), channel_id=1, source_target_pairs={{8,0},{16,8},{24,16},{32,24},{40,32},{48,40},{56,48},{64,56},{72,6... | collective-permute-start | bytes 221192 | tf_op jit(solution)/shard_map/ppermute | solution.py:28
  252.9 7.8 %collective-permute-start.8 = (bf16[3,1,48,256]{3,2,1,0:T(8,128)(2,1)S(1)}, bf16[3,1,48,256]{3,2,1,0:T(8,128)(2,1)S(1)}, u32[]{:S(2)}, u32[]{:S(2)}) collective-permute-start(bf16[3,1,48,256]{3,2,1,0:T(8,128)(2,1)S(1)} %get-tuple-element.151), channel_id=1, source_target_pairs={{0,8},{8,16},{16,24},{24,32},{32,40},{40,48},{48,56},{56,64},{64,7... | collective-permute-start | bytes 221192 | tf_op jit(solution)/shard_map/ppermute | solution.py:27
  260.7 10.1 %collective-permute-start.11 = (bf16[3,6,1,256]{3,2,1,0:T(2,128)(2,1)S(1)}, bf16[3,6,1,256]{3,2,1,0:T(2,128)(2,1)S(1)}, u32[]{:S(2)}, u32[]{:S(2)}) collective-permute-start(bf16[3,6,1,256]{3,2,1,0:T(2,128)(2,1)S(1)} %get-tuple-element.145), channel_id=1, source_target_pairs={{1,0},{2,1},{3,2},{4,3},{5,4},{6,5},{7,6},{9,8},{10,9},{11,10},{12... | collective-permute-start | bytes 27656 | tf_op jit(solution)/shard_map/ppermute | solution.py:28
  262.6 9.0 %collective-permute-start.10 = (bf16[3,6,1,256]{3,2,1,0:T(2,128)(2,1)S(1)}, bf16[3,6,1,256]{3,2,1,0:T(2,128)(2,1)S(1)}, u32[]{:S(2)}, u32[]{:S(2)}) collective-permute-start(bf16[3,6,1,256]{3,2,1,0:T(2,128)(2,1)S(1)} %get-tuple-element.144), channel_id=1, source_target_pairs={{0,1},{1,2},{2,3},{3,4},{4,5},{5,6},{6,7},{8,9},{9,10},{10,11},{11... | collective-permute-start | bytes 27656 | tf_op jit(solution)/shard_map/ppermute | solution.py:27
Sparse Core Ops, SparseCore 0:
  35.6 43.2 all-gather.1
  151.4 32.9 reduce-scatter.6
  186.9 34.2 reduce-scatter.4

commit v3 on v2

--- a/solution.py
+++ b/solution.py
@@ -158,12 +158,18 @@
         scale,
     )
     top, total, acc, along_y, along_x = carry
-    peak = lax.pmax(top, QUERY_AXES)
-    factor = jnp.exp(top - peak)
-    acc = lax.psum_scatter(acc * factor[:, None], QUERY_AXES, scatter_dimension=0, tiled=True)
-    stats = jnp.stack([total * factor, along_y * factor, along_x * factor])
-    stats = lax.psum_scatter(stats, QUERY_AXES, scatter_dimension=1, tiled=True)
-    total, along_y, along_x = stats[0], stats[1], stats[2]
+    parts = lax.axis_size(QUERY_AXES)
+    stats = jnp.stack([top, total, along_y, along_x]).reshape(4, parts, tokens)
+    stats = jnp.pad(stats.transpose(1, 0, 2), ((0, 0), (0, 0), (0, width - tokens)))
+    packed = jnp.concatenate([acc.reshape(parts, tokens, width), stats], axis=1)
+    packed = lax.all_to_all(packed, QUERY_AXES, 0, 0, tiled=True)
+    tops = packed[:, tokens, :tokens]
+    peak = jnp.max(tops, axis=0)
+    factor = jnp.exp(tops - peak[None])
+    acc = jnp.sum(packed[:, :tokens, :] * factor[:, :, None], axis=0)
+    total = jnp.sum(packed[:, tokens + 1, :tokens] * factor, axis=0)
+    along_y = jnp.sum(packed[:, tokens + 2, :tokens] * factor, axis=0)
+    along_x = jnp.sum(packed[:, tokens + 3, :tokens] * factor, axis=0)
     warped = (acc / total[:, None]).astype(jnp.bfloat16).reshape(rows, cols, width)
     own_y = norm_y(row_start + jnp.arange(rows, dtype=jnp.int32))
     own_x = norm_x(col_start + jnp.arange(cols, dtype=jnp.int32))

time: 283 us -> 234 us (0.83)
  waiting for transfers between devices: 101 us -> 61 us
  blocking collectives: 52.7 us -> 41.9 us
  starting transfers between devices: 41.2 us -> 45.5 us
    unnamed x4 -> x1, waiting for transfers between devices: 31.6 us -> 0.02 us
    reduce_scatter x1 -> x0, waiting for transfers between devices: 28.6 us -> none  [body(): lax.psum_scatter(acc * factor[:, None], QUERY_AXES, scatter_dimension=0,...]
    all_to_all x0 -> x1, waiting for transfers between devices: none -> 20.1 us  [body(): packed = lax.all_to_all(packed, QUERY_AXES, 0, 0, tiled=True)]
    pmax x1 -> x0, blocking collectives: 10.8 us -> none  [body(): peak = lax.pmax(top, QUERY_AXES)]
    all_to_all x0 -> x1, starting transfers between devices: none -> 4.91 us  [body(): packed = lax.all_to_all(packed, QUERY_AXES, 0, 0, tiled=True)]
  transfers between devices with their start and end apart: 15 -> 14, of which waited for: 6 -> 5; matrix products, arithmetic and copies ran while one was open for 3% -> 2% of each run, Pallas kernels for 0% -> 0%
where the time goes in v3:
time: 234 us; the launch traced here: 230 us
  waiting for transfers between devices  61 us (26%)
  starting transfers between devices  45.5 us (19%)
  blocking collectives  41.9 us (18%)
  matrix products  34.6 us (15%)
  other arithmetic  31.7 us (14%)
  between operations  14.4 us (6%)
    all_gather x1, waiting for transfers between devices, body(): piece = lax.all_gather(piece, axis, axis=0, tiled=True)  29.3 us
    all_gather x1, blocking collectives, body(): piece = lax.all_gather(piece, axis, axis=0, tiled=True)  28.3 us
    reduce_sum x3, other arithmetic, visit(): along_x = along_x * shrink + jnp.sum(expo * block_x[None, :], axis=1)  25.5 us
    ppermute x6, starting transfers between devices, with_halo(): before = lax.ppermute(last, axis, up)  23.7 us
    dot_general x3, matrix products, visit(): lax.dot_general(queries, key_block, (((1,), (1,)), ((), ())), preferred_e...  22.8 us
    all_to_all x1, waiting for transfers between devices, body(): packed = lax.all_to_all(packed, QUERY_AXES, 0, 0, tiled=True)  20.1 us
    ppermute x6, starting transfers between devices, with_halo(): after = lax.ppermute(first, axis, down)  16.9 us
    all_gather x1, blocking collectives, body(): lax.all_gather(feat1.reshape(tokens, width), QUERY_AXES, axis=0, tiled=True)  13.6 us
  transfers between devices with their start and end apart: 14, of which 5 were waited for; matrix products, arithmetic and copies ran while one was open for 2% of the time, Pallas kernels for 0%

profile of v3, /device:TPU:152, one launch (start us, length us, event | category | flops | bytes accessed | tf_op | source)
XLA Modules:
  0.0 230.4 jit_solution(6486698609514709676)
XLA Ops:
  7.2 0.0 all-gather.2.cloned.1.call-start
  7.2 28.3 %all_gather.9 = bf16[32,48,256]{2,1,0:T(8,128)(2,1)} all-gather(bf16[4,48,256]{2,1,0:T(8,128)(2,1)} %param.5), channel_id=1, replica_groups=mesh['z'=8,'xl'=2,'c'=2,'xh'=2,'y'=4] {'z'}, dimensions={0}, use_global_device_ids=true | all-gather | bytes 884736 | tf_op jit(solution)/shard_map/all_gather | solution.py:135
  35.5 0.0 all-gather.2.cloned.1.call-update
  35.6 0.1 broadcast_in_dim.34
  35.7 0.1 sub.129
  35.8 0.1 multiply_add_fusion.2
  35.9 0.1 reshape.310
  36.0 13.6 %all_gather.11 = bf16[1536,256]{1,0:T(8,128)(2,1)S(1)} all-gather(bf16[192,256]{1,0:T(8,128)(2,1)} %bitcast.82), channel_id=1, replica_groups=mesh['z'=8,'xl'=2,'c'=2,'xh'=2,'y'=4] {'y','c'}, dimensions={0}, use_global_device_ids=true | all-gather | bytes 884736 | tf_op jit(solution)/shard_map/all_gather | solution.py:117
  49.6 29.3 %all-gather.2.cloned.1.call-done = bf16[128,48,256]{2,1,0:T(8,128)(2,1)} async-done(((bf16[32,48,256]{2,1,0:T(8,128)(2,1)}), bf16[128,48,256]{2,1,0:T(8,128)(2,1)}) %all-gather.2.cloned.1.call-update) | async-done | bytes 3145744 | tf_op jit(solution)/shard_map/all_gather | solution.py:135
  78.9 60.4 %while.19 = (s32[]{:T(128)}, f32[1536]{0:T(1024)S(1)}, f32[1536]{0:T(1024)S(1)}, f32[1536,256]{1,0:T(8,128)S(1)}, f32[1536]{0:T(1024)S(1)}, /*index=5*/f32[1536]...) while((s32[]{:T(128)}, f32[1536]{0:T(1024)S(1)}, ...), condition=%wide.region_5.6_spmd.clone, body=%wide.region_0.5_spmd.clone.sunk | while | flops 3260167680 | bytes 94312616 | solution.py:104
  79.0 7.6 %multiply_reduce_fusion.5 = (f32[1536]{0:T(1024)S(1)}, f32[2048,1536]{1,0:T(8,128)}) fusion(bf16[1536,256]{1,0:T(8,128)(2,1)S(1)} %get-tuple-element.282, bf16[3,2048,256]{2,1,0:T(8,128)(2,1)} %get-tuple-element.281, s32[]{:T(128)S(6)} %copy.42), kind=kOutput, calls=%fused_computation.3.clone.1 | convolution fusion | flops 1616902656 | bytes 14424068 | tf_op jit(solution)/shard_map/while/body/eval_jaxpr/dot_general | solution.py:83
  86.6 8.5 %multiply_reduce_fusion.6 = (f32[1536]{0:T(1024)S(1)}, f32[1536]{0:T(1024)S(1)}, f32[1536]{0:T(1024)S(1)}) fusion(f32[2048]{0:T(1024)S(1)} %bitcast.89, f32[1536]{0:T(1024)S(1)} %select_maximum_fusion.3, f32[2048,1536]{1,0:T(8,128)} %get-tuple-element.242, f32[2048]{0:T(1024)S(1)} %bitcast.90), kind=kLoop, calls=%fused_computation.clone.1 | loop fusion | flops 22015488 | bytes 12623872 | tf_op jit(solution)/shard_map/while/body/eval_jaxpr/reduce_sum | solution.py:96
  95.1 3.9 %fusion.89 = f32[1536,256]{1,0:T(8,128)S(1)} fusion(f32[1536]{0:T(1024)S(1)} %select_maximum_fusion.3, f32[2048,1536]{1,0:T(8,128)S(1)} %copy-done, f32[1536,256]{1,0:T(8,128)S(1)} %get-tuple-element.266, bf16[3,2048,256]{2,1,0:T(8,128)(2,1)} %get-tuple-element.281, s32[]{:T(128)S(6)} %copy.42, f32[1536]{0:T(1024)S(1)} %get-tuple-element.246, ...), kind=kOutput, calls=%fused_computation.7.clone.1 | convolution fusion | flops 1621229568 | bytes 16789508 | tf_op jit(solution)/shard_map/while/body/eval_jaxpr/dot_general | solution.py:92
  99.1 7.6 %multiply_reduce_fusion.5 = (f32[1536]{0:T(1024)S(1)}, f32[2048,1536]{1,0:T(8,128)}) fusion(bf16[1536,256]{1,0:T(8,128)(2,1)S(1)} %get-tuple-element.282, bf16[3,2048,256]{2,1,0:T(8,128)(2,1)} %get-tuple-element.281, s32[]{:T(128)S(6)} %copy.42), kind=kOutput, calls=%fused_computation.3.clone.1 | convolution fusion | flops 1616902656 | bytes 14424068 | tf_op jit(solution)/shard_map/while/body/eval_jaxpr/dot_general | solution.py:83
  106.7 8.5 %multiply_reduce_fusion.6 = (f32[1536]{0:T(1024)S(1)}, f32[1536]{0:T(1024)S(1)}, f32[1536]{0:T(1024)S(1)}) fusion(f32[2048]{0:T(1024)S(1)} %bitcast.89, f32[1536]{0:T(1024)S(1)} %select_maximum_fusion.3, f32[2048,1536]{1,0:T(8,128)} %get-tuple-element.242, f32[2048]{0:T(1024)S(1)} %bitcast.90), kind=kLoop, calls=%fused_computation.clone.1 | loop fusion | flops 22015488 | bytes 12623872 | tf_op jit(solution)/shard_map/while/body/eval_jaxpr/reduce_sum | solution.py:96
  115.3 3.9 %fusion.89 = f32[1536,256]{1,0:T(8,128)S(1)} fusion(f32[1536]{0:T(1024)S(1)} %select_maximum_fusion.3, f32[2048,1536]{1,0:T(8,128)S(1)} %copy-done, f32[1536,256]{1,0:T(8,128)S(1)} %get-tuple-element.266, bf16[3,2048,256]{2,1,0:T(8,128)(2,1)} %get-tuple-element.281, s32[]{:T(128)S(6)} %copy.42, f32[1536]{0:T(1024)S(1)} %get-tuple-element.246, ...), kind=kOutput, calls=%fused_computation.7.clone.1 | convolution fusion | flops 1621229568 | bytes 16789508 | tf_op jit(solution)/shard_map/while/body/eval_jaxpr/dot_general | solution.py:92
  119.2 7.6 %multiply_reduce_fusion.5 = (f32[1536]{0:T(1024)S(1)}, f32[2048,1536]{1,0:T(8,128)}) fusion(bf16[1536,256]{1,0:T(8,128)(2,1)S(1)} %get-tuple-element.282, bf16[3,2048,256]{2,1,0:T(8,128)(2,1)} %get-tuple-element.281, s32[]{:T(128)S(6)} %copy.42), kind=kOutput, calls=%fused_computation.3.clone.1 | convolution fusion | flops 1616902656 | bytes 14424068 | tf_op jit(solution)/shard_map/while/body/eval_jaxpr/dot_general | solution.py:83
  126.9 8.5 %multiply_reduce_fusion.6 = (f32[1536]{0:T(1024)S(1)}, f32[1536]{0:T(1024)S(1)}, f32[1536]{0:T(1024)S(1)}) fusion(f32[2048]{0:T(1024)S(1)} %bitcast.89, f32[1536]{0:T(1024)S(1)} %select_maximum_fusion.3, f32[2048,1536]{1,0:T(8,128)} %get-tuple-element.242, f32[2048]{0:T(1024)S(1)} %bitcast.90), kind=kLoop, calls=%fused_computation.clone.1 | loop fusion | flops 22015488 | bytes 12623872 | tf_op jit(solution)/shard_map/while/body/eval_jaxpr/reduce_sum | solution.py:96
  135.4 3.9 %fusion.89 = f32[1536,256]{1,0:T(8,128)S(1)} fusion(f32[1536]{0:T(1024)S(1)} %select_maximum_fusion.3, f32[2048,1536]{1,0:T(8,128)S(1)} %copy-done, f32[1536,256]{1,0:T(8,128)S(1)} %get-tuple-element.266, bf16[3,2048,256]{2,1,0:T(8,128)(2,1)} %get-tuple-element.281, s32[]{:T(128)S(6)} %copy.42, f32[1536]{0:T(1024)S(1)} %get-tuple-element.246, ...), kind=kOutput, calls=%fused_computation.7.clone.1 | convolution fusion | flops 1621229568 | bytes 16789508 | tf_op jit(solution)/shard_map/while/body/eval_jaxpr/dot_general | solution.py:92
  139.4 0.1 stack.45
  139.4 0.1 stack.44
  139.5 0.1 stack.43
  139.6 0.1 stack.42
  139.7 1.3 select_maximum_fusion.1
  141.1 4.9 %all-to-all-start = ((f32[8,196,256]{2,1,0:T(8,128)}), f32[8,196,256]{2,1,0:T(8,128)S(1)}, u32[]{:S(2)}, u32[]{:S(2)}) async-start(f32[8,196,256]{2,1,0:T(8,128)} %select_maximum_fusion.1), calls=%async_computation | async-start | bytes 3276800 | tf_op jit(solution)/shard_map/all_to_all | solution.py:165
  146.0 20.1 %all-to-all-done = f32[8,196,256]{2,1,0:T(8,128)S(1)} async-done(((f32[8,196,256]{2,1,0:T(8,128)}), f32[8,196,256]{2,1,0:T(8,128)S(1)}, u32[]{:S(2)}, u32[]{:S(2)}) %all-to-all-start) | async-done | bytes 1605664 | tf_op jit(solution)/shard_map/all_to_all | solution.py:165
  166.3 0.1 div.142
  166.3 0.1 div.141
  166.4 0.1 div.139
  166.5 0.1 broadcast_subtract_fusion
  166.6 1.9 collective-permute-start.4
  168.5 2.4 %collective-permute-start.5 = (f32[2,1,48]{2,1,0:T(1,128)S(1)}, f32[2,1,48]{2,1,0:T(1,128)S(1)}, u32[]{:S(2)}, u32[]{:S(2)}) collective-permute-start(f32[2,1,48]{2,1,0:T(1,128)S(1)} %get-tuple-element.162), channel_id=1, source_target_pairs={{0,8},{8,16},{16,24},{24,32},{32,40},{40,48},{48,56},{56,64},{64,7... | collective-permute-start | bytes 1160 | tf_op jit(solution)/shard_map/ppermute | solution.py:27
  170.9 0.3 fusion.17
  171.2 0.1 divide_convert_fusion.1
  171.3 0.6 pad_maximum_fusion.16
  171.9 5.3 %collective-permute-start.1 = (bf16[2,1,48,256]{3,2,1,0:T(8,128)(2,1)S(1)}, bf16[2,1,48,256]{3,2,1,0:T(8,128)(2,1)S(1)}, u32[]{:S(2)}, u32[]{:S(2)}) collective-permute-start(bf16[2,1,48,256]{3,2,1,0:T(8,128)(2,1)S(1)} %get-tuple-element.159), channel_id=1, source_target_pairs={{8,0},{16,8},{24,16},{32,24},{40,32},{48,40},{56,48},{64,56},{72,6... | collective-permute-start | bytes 147464 | tf_op jit(solution)/shard_map/ppermute | solution.py:28
  177.2 1.9 collective-permute-start
  179.1 0.0 collective-permute-done.5
  179.2 5.5 %collective-permute-done = bf16[2,1,48,256]{3,2,1,0:T(8,128)(2,1)S(1)} collective-permute-done((bf16[2,1,48,256]{3,2,1,0:T(8,128)(2,1)S(1)}, bf16[2,1,48,256]{3,2,1,0:T(8,128)(2,1)S(1)}, u32[]{:S(2)}, u32[]{:S(2)}) %collective-permute-start) | collective-permute-done | bytes 49184 | tf_op jit(solution)/shard_map/ppermute | solution.py:27
  184.8 1.9 collective-permute-start.3
  186.7 7.5 %collective-permute-start.2 = (bf16[2,6,1,256]{3,2,1,0:T(2,128)(2,1)S(1)}, bf16[2,6,1,256]{3,2,1,0:T(2,128)(2,1)S(1)}, u32[]{:S(2)}, u32[]{:S(2)}) collective-permute-start(bf16[2,6,1,256]{3,2,1,0:T(2,128)(2,1)S(1)} %get-tuple-element.156), channel_id=1, source_target_pairs={{0,1},{1,2},{2,3},{3,4},{4,5},{5,6},{6,7},{8,9},{9,10},{10,11},{11... | collective-permute-start | bytes 18440 | tf_op jit(solution)/shard_map/ppermute | solution.py:27
  194.2 0.1 fusion.75
  194.3 1.9 collective-permute-start.7
  196.2 3.9 %collective-permute-start.6 = (f32[2,6,1]{2,1,0:T(8,128)S(1)}, f32[2,6,1]{2,1,0:T(8,128)S(1)}, u32[]{:S(2)}, u32[]{:S(2)}) collective-permute-start(f32[2,6,1]{2,1,0:T(8,128)S(1)} %get-tuple-element.160), channel_id=1, source_target_pairs={{1,0},{2,1},{3,2},{4,3},{5,4},{6,5},{7,6},{9,8},{10,9},{11,10},{12... | collective-permute-start | bytes 152 | tf_op jit(solution)/shard_map/ppermute | solution.py:28
  200.1 0.0 collective-permute-done.3
  200.2 0.1 pad_maximum_fusion
  200.3 0.1 fusion.44
  200.4 0.1 fusion.21
  200.5 0.1 fusion.19
  200.6 0.1 fusion.47
  200.7 0.8 fusion.51
  201.5 0.1 convert_bitcast_fusion
  201.7 1.9 collective-permute-start.9
  203.6 2.4 %collective-permute-start.8 = (bf16[3,1,48,256]{3,2,1,0:T(8,128)(2,1)S(1)}, bf16[3,1,48,256]{3,2,1,0:T(8,128)(2,1)S(1)}, u32[]{:S(2)}, u32[]{:S(2)}) collective-permute-start(bf16[3,1,48,256]{3,2,1,0:T(8,128)(2,1)S(1)} %get-tuple-element.154), channel_id=1, source_target_pairs={{0,8},{8,16},{16,24},{24,32},{32,40},{40,48},{48,56},{56,64},{64,7... | collective-permute-start | bytes 221192 | tf_op jit(solution)/shard_map/ppermute | solution.py:27
  206.0 0.1 multiply_select_fusion
  206.1 0.1 multiply_select_fusion.1
  206.2 5.2 %collective-permute-done.8 = bf16[3,1,48,256]{3,2,1,0:T(8,128)(2,1)S(1)} collective-permute-done((bf16[3,1,48,256]{3,2,1,0:T(8,128)(2,1)S(1)}, bf16[3,1,48,256]{3,2,1,0:T(8,128)(2,1)S(1)}, u32[]{:S(2)}, u32[]{:S(2)}) %collective-permute-start.8) | collective-permute-done | bytes 73760 | tf_op jit(solution)/shard_map/ppermute | solution.py:27
  211.4 1.9 collective-permute-start.11
  213.3 7.5 %collective-permute-start.10 = (bf16[3,6,1,256]{3,2,1,0:T(2,128)(2,1)S(1)}, bf16[3,6,1,256]{3,2,1,0:T(2,128)(2,1)S(1)}, u32[]{:S(2)}, u32[]{:S(2)}) collective-permute-start(bf16[3,6,1,256]{3,2,1,0:T(2,128)(2,1)S(1)} %get-tuple-element.147), channel_id=1, source_target_pairs={{0,1},{1,2},{2,3},{3,4},{4,5},{5,6},{6,7},{8,9},{9,10},{10,11},{11... | collective-permute-start | bytes 27656 | tf_op jit(solution)/shard_map/ppermute | solution.py:27
  220.9 0.7 slice_subtract_fusion.2
  221.6 0.8 collective-permute-done.10
  222.3 0.1 maximum_convert_fusion
  222.5 0.1 slice_bitcast_fusion.2
  222.6 1.0 fusion.24
  (53 shorter events, 0.5 us)
Async XLA Ops:
  7.2 71.8 %all-gather.2.cloned.1.call-start = ((), (), s32[]{:S(2)}) async-start(), calls=%async_computation.1 | async-start | bytes 3932160 | tf_op jit(solution)/shard_map/all_gather | solution.py:135
  86.6 8.5 %copy-start = (f32[2048,1536]{1,0:T(8,128)S(1)}, f32[2048,1536]{1,0:T(8,128)}, u32[]{:S(2)}) copy-start(f32[2048,1536]{1,0:T(8,128)} %get-tuple-element.242) | copy-start | bytes 37748740 | tf_op jit(solution)/shard_map/while
  106.7 8.5 %copy-start = (f32[2048,1536]{1,0:T(8,128)S(1)}, f32[2048,1536]{1,0:T(8,128)}, u32[]{:S(2)}) copy-start(f32[2048,1536]{1,0:T(8,128)} %get-tuple-element.242) | copy-start | bytes 37748740 | tf_op jit(solution)/shard_map/while
  126.9 8.5 %copy-start = (f32[2048,1536]{1,0:T(8,128)S(1)}, f32[2048,1536]{1,0:T(8,128)}, u32[]{:S(2)}) copy-start(f32[2048,1536]{1,0:T(8,128)} %get-tuple-element.242) | copy-start | bytes 37748740 | tf_op jit(solution)/shard_map/while
  141.1 30.2 %copy-start.1 = (bf16[4,48,256]{2,1,0:T(8,128)(2,1)S(1)}, bf16[4,48,256]{2,1,0:T(8,128)(2,1)}, u32[]{:S(2)}) copy-start(bf16[4,48,256]{2,1,0:T(8,128)(2,1)} %param.4) | copy-start | bytes 294916
  141.1 25.1 %all-to-all-start = ((f32[8,196,256]{2,1,0:T(8,128)}), f32[8,196,256]{2,1,0:T(8,128)S(1)}, u32[]{:S(2)}, u32[]{:S(2)}) async-start(f32[8,196,256]{2,1,0:T(8,128)} %select_maximum_fusion.1), calls=%async_computation | async-start | bytes 3276800 | tf_op jit(solution)/shard_map/all_to_all | solution.py:165
  166.6 12.5 %collective-permute-start.4 = (f32[2,1,48]{2,1,0:T(1,128)S(1)}, f32[2,1,48]{2,1,0:T(1,128)S(1)}, u32[]{:S(2)}, u32[]{:S(2)}) collective-permute-start(f32[2,1,48]{2,1,0:T(1,128)S(1)} %get-tuple-element.163), channel_id=1, source_target_pairs={{8,0},{16,8},{24,16},{32,24},{40,32},{48,40},{56,48},{64,56},{72,6... | collective-permute-start | bytes 1160 | tf_op jit(solution)/shard_map/ppermute | solution.py:28
  168.5 10.6 %collective-permute-start.5 = (f32[2,1,48]{2,1,0:T(1,128)S(1)}, f32[2,1,48]{2,1,0:T(1,128)S(1)}, u32[]{:S(2)}, u32[]{:S(2)}) collective-permute-start(f32[2,1,48]{2,1,0:T(1,128)S(1)} %get-tuple-element.162), channel_id=1, source_target_pairs={{0,8},{8,16},{16,24},{24,32},{32,40},{40,48},{48,56},{56,64},{64,7... | collective-permute-start | bytes 1160 | tf_op jit(solution)/shard_map/ppermute | solution.py:27
  171.9 7.2 %collective-permute-start.1 = (bf16[2,1,48,256]{3,2,1,0:T(8,128)(2,1)S(1)}, bf16[2,1,48,256]{3,2,1,0:T(8,128)(2,1)S(1)}, u32[]{:S(2)}, u32[]{:S(2)}) collective-permute-start(bf16[2,1,48,256]{3,2,1,0:T(8,128)(2,1)S(1)} %get-tuple-element.159), channel_id=1, source_target_pairs={{8,0},{16,8},{24,16},{32,24},{40,32},{48,40},{56,48},{64,56},{72,6... | collective-permute-start | bytes 147464 | tf_op jit(solution)/shard_map/ppermute | solution.py:28
  177.2 7.5 %collective-permute-start = (bf16[2,1,48,256]{3,2,1,0:T(8,128)(2,1)S(1)}, bf16[2,1,48,256]{3,2,1,0:T(8,128)(2,1)S(1)}, u32[]{:S(2)}, u32[]{:S(2)}) collective-permute-start(bf16[2,1,48,256]{3,2,1,0:T(8,128)(2,1)S(1)} %get-tuple-element.158), channel_id=1, source_target_pairs={{0,8},{8,16},{16,24},{24,32},{32,40},{40,48},{48,56},{56,64},{64,7... | collective-permute-start | bytes 147464 | tf_op jit(solution)/shard_map/ppermute | solution.py:27
  184.8 15.4 %collective-permute-start.3 = (bf16[2,6,1,256]{3,2,1,0:T(2,128)(2,1)S(1)}, bf16[2,6,1,256]{3,2,1,0:T(2,128)(2,1)S(1)}, u32[]{:S(2)}, u32[]{:S(2)}) collective-permute-start(bf16[2,6,1,256]{3,2,1,0:T(2,128)(2,1)S(1)} %get-tuple-element.157), channel_id=1, source_target_pairs={{1,0},{2,1},{3,2},{4,3},{5,4},{6,5},{7,6},{9,8},{10,9},{11,10},{12... | collective-permute-start | bytes 18440 | tf_op jit(solution)/shard_map/ppermute | solution.py:28
  186.7 13.5 %collective-permute-start.2 = (bf16[2,6,1,256]{3,2,1,0:T(2,128)(2,1)S(1)}, bf16[2,6,1,256]{3,2,1,0:T(2,128)(2,1)S(1)}, u32[]{:S(2)}, u32[]{:S(2)}) collective-permute-start(bf16[2,6,1,256]{3,2,1,0:T(2,128)(2,1)S(1)} %get-tuple-element.156), channel_id=1, source_target_pairs={{0,1},{1,2},{2,3},{3,4},{4,5},{5,6},{6,7},{8,9},{9,10},{10,11},{11... | collective-permute-start | bytes 18440 | tf_op jit(solution)/shard_map/ppermute | solution.py:27
  194.3 11.8 %collective-permute-start.7 = (f32[2,6,1]{2,1,0:T(8,128)S(1)}, f32[2,6,1]{2,1,0:T(8,128)S(1)}, u32[]{:S(2)}, u32[]{:S(2)}) collective-permute-start(f32[2,6,1]{2,1,0:T(8,128)S(1)} %get-tuple-element.161), channel_id=1, source_target_pairs={{0,1},{1,2},{2,3},{3,4},{4,5},{5,6},{6,7},{8,9},{9,10},{10,11},{11... | collective-permute-start | bytes 152 | tf_op jit(solution)/shard_map/ppermute | solution.py:27
  196.2 9.9 %collective-permute-start.6 = (f32[2,6,1]{2,1,0:T(8,128)S(1)}, f32[2,6,1]{2,1,0:T(8,128)S(1)}, u32[]{:S(2)}, u32[]{:S(2)}) collective-permute-start(f32[2,6,1]{2,1,0:T(8,128)S(1)} %get-tuple-element.160), channel_id=1, source_target_pairs={{1,0},{2,1},{3,2},{4,3},{5,4},{6,5},{7,6},{9,8},{10,9},{11,10},{12... | collective-permute-start | bytes 152 | tf_op jit(solution)/shard_map/ppermute | solution.py:28
  201.7 4.5 %collective-permute-start.9 = (bf16[3,1,48,256]{3,2,1,0:T(8,128)(2,1)S(1)}, bf16[3,1,48,256]{3,2,1,0:T(8,128)(2,1)S(1)}, u32[]{:S(2)}, u32[]{:S(2)}) collective-permute-start(bf16[3,1,48,256]{3,2,1,0:T(8,128)(2,1)S(1)} %get-tuple-element.155), channel_id=1, source_target_pairs={{8,0},{16,8},{24,16},{32,24},{40,32},{48,40},{56,48},{64,56},{72,6... | collective-permute-start | bytes 221192 | tf_op jit(solution)/shard_map/ppermute | solution.py:28
  203.6 7.8 %collective-permute-start.8 = (bf16[3,1,48,256]{3,2,1,0:T(8,128)(2,1)S(1)}, bf16[3,1,48,256]{3,2,1,0:T(8,128)(2,1)S(1)}, u32[]{:S(2)}, u32[]{:S(2)}) collective-permute-start(bf16[3,1,48,256]{3,2,1,0:T(8,128)(2,1)S(1)} %get-tuple-element.154), channel_id=1, source_target_pairs={{0,8},{8,16},{16,24},{24,32},{32,40},{40,48},{48,56},{56,64},{64,7... | collective-permute-start | bytes 221192 | tf_op jit(solution)/shard_map/ppermute | solution.py:27
  211.4 10.1 %collective-permute-start.11 = (bf16[3,6,1,256]{3,2,1,0:T(2,128)(2,1)S(1)}, bf16[3,6,1,256]{3,2,1,0:T(2,128)(2,1)S(1)}, u32[]{:S(2)}, u32[]{:S(2)}) collective-permute-start(bf16[3,6,1,256]{3,2,1,0:T(2,128)(2,1)S(1)} %get-tuple-element.148), channel_id=1, source_target_pairs={{1,0},{2,1},{3,2},{4,3},{5,4},{6,5},{7,6},{9,8},{10,9},{11,10},{12... | collective-permute-start | bytes 27656 | tf_op jit(solution)/shard_map/ppermute | solution.py:28
  213.3 9.0 %collective-permute-start.10 = (bf16[3,6,1,256]{3,2,1,0:T(2,128)(2,1)S(1)}, bf16[3,6,1,256]{3,2,1,0:T(2,128)(2,1)S(1)}, u32[]{:S(2)}, u32[]{:S(2)}) collective-permute-start(bf16[3,6,1,256]{3,2,1,0:T(2,128)(2,1)S(1)} %get-tuple-element.147), channel_id=1, source_target_pairs={{0,1},{1,2},{2,3},{3,4},{4,5},{5,6},{6,7},{8,9},{9,10},{10,11},{11... | collective-permute-start | bytes 27656 | tf_op jit(solution)/shard_map/ppermute | solution.py:27
Sparse Core Ops, SparseCore 0:
  35.6 43.2 all-gather.1

commit v4 on v3

--- a/solution.py
+++ b/solution.py
@@ -3,6 +3,8 @@
 import jax
 import jax.numpy as jnp
 from jax import lax
+from jax.experimental import pallas as pl
+from jax.experimental.pallas import tpu as pltpu
 from jax.sharding import Mesh
 from jax.sharding import PartitionSpec as P
 
@@ -15,6 +17,8 @@
 COL = ("xh", "y")
 KEY_AXES = ("z", ("xh", "xl"))
 QUERY_AXES = ("y", "c")
+BLOCK_Q = 512
+BLOCK_K = 1024
 
 
 def with_halo(value, sides, width):
@@ -68,41 +72,75 @@
     return weight * delta / jnp.sqrt(delta * delta + charb_sq)
 
 
-def absorb(carry, queries, keys, key_y, key_x, scale):
-    total_keys = keys.shape[0]
-    width = keys.shape[1]
-    step = min(total_keys, 2048)
-    while total_keys % step != 0:
-        step = step - 1
-    blocks = total_keys // step
-
-    def visit(state, item):
-        top, total, acc, along_y, along_x = state
-        key_block, block_y, block_x = item
-        score = (
-            lax.dot_general(
-                queries, key_block, (((1,), (1,)), ((), ())), preferred_element_type=jnp.float32
-            )
-            * scale
-        )
-        new_top = jnp.maximum(top, jnp.max(score, axis=1))
-        shrink = jnp.exp(top - new_top)
-        expo = jnp.exp(score - new_top[:, None])
-        total = total * shrink + jnp.sum(expo, axis=1)
-        acc = acc * shrink[:, None] + jnp.dot(
-            expo.astype(jnp.bfloat16), key_block, preferred_element_type=jnp.float32
-        )
-        along_y = along_y * shrink + jnp.sum(expo * block_y[None, :], axis=1)
-        along_x = along_x * shrink + jnp.sum(expo * block_x[None, :], axis=1)
-        return ((new_top, total, acc, along_y, along_x), None)
-
-    items = (
-        keys.reshape(blocks, step, width),
-        key_y.reshape(blocks, step),
-        key_x.reshape(blocks, step),
-    )
-    carry, unused = lax.scan(visit, carry, items)
-    return carry
+def flash_partials(queries, keys, key_y, key_x, scale, block_q, block_k):
+    nq, width = queries.shape
+    nk = keys.shape[0]
+    grid = (nq // block_q, nk // block_k)
+    last = grid[1] - 1
+
+    def kernel(q_ref, k_ref, y_ref, x_ref, top_ref, total_ref, acc_ref, ay_ref, ax_ref,
+               m_sc, l_sc, acc_sc, ay_sc, ax_sc):
+        step = pl.program_id(1)
+
+        @pl.when(step == 0)
+        def _():
+            m_sc[...] = jnp.full(m_sc.shape, -1e30, jnp.float32)
+            l_sc[...] = jnp.zeros(l_sc.shape, jnp.float32)
+            acc_sc[...] = jnp.zeros(acc_sc.shape, jnp.float32)
+            ay_sc[...] = jnp.zeros(ay_sc.shape, jnp.float32)
+            ax_sc[...] = jnp.zeros(ax_sc.shape, jnp.float32)
+
+        k = k_ref[...]
+        score = lax.dot_general(q_ref[...], k, (((1,), (1,)), ((), ())),
+                                preferred_element_type=jnp.float32) * scale
+        m_prev = m_sc[...]
+        m_new = jnp.maximum(m_prev, jnp.max(score, axis=1, keepdims=True))
+        shrink = jnp.exp(m_prev - m_new)
+        expo = jnp.exp(score - m_new)
+        l_sc[...] = l_sc[...] * shrink + jnp.sum(expo, axis=1, keepdims=True)
+        ay_sc[...] = ay_sc[...] * shrink + jnp.sum(expo * y_ref[...], axis=1, keepdims=True)
+        ax_sc[...] = ax_sc[...] * shrink + jnp.sum(expo * x_ref[...], axis=1, keepdims=True)
+        acc_sc[...] = acc_sc[...] * shrink + jnp.dot(expo.astype(jnp.bfloat16), k,
+                                                     preferred_element_type=jnp.float32)
+        m_sc[...] = m_new
+
+        @pl.when(step == last)
+        def _():
+            top_ref[...] = m_sc[...]
+            total_ref[...] = l_sc[...]
+            acc_ref[...] = acc_sc[...]
+            ay_ref[...] = ay_sc[...]
+            ax_ref[...] = ax_sc[...]
+
+    col = pl.BlockSpec((block_q, 1), lambda i, j: (i, 0))
+    outs = pl.pallas_call(
+        kernel,
+        grid=grid,
+        in_specs=[
+            pl.BlockSpec((block_q, width), lambda i, j: (i, 0)),
+            pl.BlockSpec((block_k, width), lambda i, j: (j, 0)),
+            pl.BlockSpec((1, block_k), lambda i, j: (0, j)),
+            pl.BlockSpec((1, block_k), lambda i, j: (0, j)),
+        ],
+        out_specs=[col, col, pl.BlockSpec((block_q, width), lambda i, j: (i, 0)), col, col],
+        out_shape=[
+            jax.ShapeDtypeStruct((nq, 1), jnp.float32),
+            jax.ShapeDtypeStruct((nq, 1), jnp.float32),
+            jax.ShapeDtypeStruct((nq, width), jnp.float32),
+            jax.ShapeDtypeStruct((nq, 1), jnp.float32),
+            jax.ShapeDtypeStruct((nq, 1), jnp.float32),
+        ],
+        scratch_shapes=[
+            pltpu.VMEM((block_q, 1), jnp.float32),
+            pltpu.VMEM((block_q, 1), jnp.float32),
+            pltpu.VMEM((block_q, width), jnp.float32),
+            pltpu.VMEM((block_q, 1), jnp.float32),
+            pltpu.VMEM((block_q, 1), jnp.float32),
+        ],
+        compiler_params=pltpu.CompilerParams(dimension_semantics=("arbitrary", "arbitrary")),
+    )(queries, keys, key_y.reshape(1, nk), key_x.reshape(1, nk))
+    top, total, acc, ay, ax = outs
+    return top[:, 0], total[:, 0], acc, ay[:, 0], ax[:, 0]
 
 
 def body(feat1, feat2):
@@ -115,14 +153,6 @@
     scale = 1.0 / math.sqrt(width)
     tokens = rows * cols
     queries = lax.all_gather(feat1.reshape(tokens, width), QUERY_AXES, axis=0, tiled=True)
-    group = queries.shape[0]
-    init = (
-        jnp.full((group,), -1e30, jnp.float32),
-        jnp.zeros((group,), jnp.float32),
-        jnp.zeros((group, width), jnp.float32),
-        jnp.zeros((group,), jnp.float32),
-        jnp.zeros((group,), jnp.float32),
-    )
 
     def norm_y(index):
         return (index.astype(jnp.float32) + 0.5) * (2.0 / full_rows) - 1.0
@@ -149,13 +179,14 @@
     tile_x = col_of * cols
     grid_y = jnp.broadcast_to(tile_y[:, None], (count, cols))
     grid_x = tile_x[:, None] + jnp.arange(cols, dtype=jnp.int32)[None, :]
-    carry = absorb(
-        init,
+    carry = flash_partials(
         queries,
         piece.reshape(count * cols, width),
         norm_y(grid_y).reshape(-1),
         norm_x(grid_x).reshape(-1),
         scale,
+        BLOCK_Q,
+        BLOCK_K,
     )
     top, total, acc, along_y, along_x = carry
     parts = lax.axis_size(QUERY_AXES)

time: 234 us -> 214 us (0.915)
  Pallas kernels: 0 us -> 38.5 us
  matrix products: 34.6 us -> 0 us
  other arithmetic: 31.7 us -> 9.69 us
  waiting for transfers between devices: 61 us -> 57.6 us
    pallas_call x0 -> x1, Pallas kernels: none -> 38.5 us  [flash_partials(): pl.pallas_call(kernel, grid=grid, in_specs=[pl.BlockSpec((block_q, width)...]
    dot_general x6 -> x0, matrix products: 34.6 us -> none  [the longest x3 22.8 us: visit(): lax.dot_general(queries, key_block, (((1,), (1,)), ((), ())), preferred_e...]
    reduce_sum x3 -> x0, other arithmetic: 25.5 us -> none  [visit(): along_x = along_x * shrink + jnp.sum(expo * block_x[None, :], axis=1)]
    ppermute x6, waiting for transfers between devices: 11.5 us -> 0.02 us  [with_halo(): before = lax.ppermute(last, axis, up)]
    ppermute x6, waiting for transfers between devices: 0.02 us -> 10.1 us  [with_halo(): after = lax.ppermute(first, axis, down)]
    pallas_call x0 -> x4, other arithmetic: none -> 3.52 us  [flash_partials(): pl.pallas_call(kernel, grid=grid, in_specs=[pl.BlockSpec((block_q, width)...]
where the time goes in v4:
time: 214 us; the launch traced here: 212 us
  waiting for transfers between devices  57.6 us (27%)
  starting transfers between devices  47 us (22%)
  blocking collectives  42.7 us (20%)
  Pallas kernels  38.5 us (18%)
  between operations  14.4 us (7%)
  other arithmetic  9.69 us (5%)
  local copies, waits for them, and re-layouts  2.26 us (1%)
    pallas_call x1, Pallas kernels, flash_partials(): pl.pallas_call(kernel, grid=grid, in_specs=[pl.BlockSpec((block_q, width)...  38.5 us
    all_gather x1, blocking collectives, body(): piece = lax.all_gather(piece, axis, axis=0, tiled=True)  28.3 us
    all_gather x1, waiting for transfers between devices, body(): piece = lax.all_gather(piece, axis, axis=0, tiled=True)  27.3 us
    ppermute x6, starting transfers between devices, with_halo(): before = lax.ppermute(last, axis, up)  23.8 us
    all_to_all x1, waiting for transfers between devices, body(): packed = lax.all_to_all(packed, QUERY_AXES, 0, 0, tiled=True)  20.1 us
    ppermute x6, starting transfers between devices, with_halo(): after = lax.ppermute(first, axis, down)  18.4 us
    all_gather x1, blocking collectives, body(): lax.all_gather(feat1.reshape(tokens, width), QUERY_AXES, axis=0, tiled=True)  14.4 us
    ppermute x6, waiting for transfers between devices, with_halo(): after = lax.ppermute(first, axis, down)  10.1 us
  transfers between devices with their start and end apart: 14, of which 5 were waited for; matrix products, arithmetic and copies ran while one was open for 2% of the time, Pallas kernels for 0%

profile of v4, /device:TPU:152, one launch (start us, length us, event | category | flops | bytes accessed | tf_op | source)
XLA Modules:
  0.0 212.1 jit_solution(5482102826396334088)
XLA Ops:
  7.2 0.0 all-gather.2.cloned.1.call-start
  7.2 28.3 %all_gather.10 = bf16[32,48,256]{2,1,0:T(8,128)(2,1)} all-gather(bf16[4,48,256]{2,1,0:T(8,128)(2,1)} %param.3), channel_id=1, replica_groups=mesh['z'=8,'xl'=2,'c'=2,'xh'=2,'y'=4] {'z'}, dimensions={0}, use_global_device_ids=true | all-gather | bytes 884736 | tf_op jit(solution)/shard_map/all_gather | solution.py:165
  35.5 0.0 all-gather.2.cloned.1.call-update
  35.6 0.1 broadcast_in_dim.24
  35.6 0.7 sub.117.y_ref
  36.4 0.1 multiply_add_fusion.2
  36.5 0.7 reshape.360.x_ref
  37.2 14.4 %all_gather.9.q_ref = bf16[1536,256]{1,0:T(8,128)(2,1)} all-gather(bf16[192,256]{1,0:T(8,128)(2,1)S(1)} %bitcast.62), channel_id=1, replica_groups=mesh['z'=8,'xl'=2,'c'=2,'xh'=2,'y'=4] {'y','c'}, dimensions={0}, use_global_device_ids=true | all-gather | bytes 884736 | tf_op jit(solution)/shard_map/all_gather | solution.py:155
  51.7 27.3 %all-gather.2.cloned.1.call-done = bf16[128,48,256]{2,1,0:T(8,128)(2,1)} async-done(((bf16[32,48,256]{2,1,0:T(8,128)(2,1)}), bf16[128,48,256]{2,1,0:T(8,128)(2,1)}) %all-gather.2.cloned.1.call-update) | async-done | bytes 3145744 | tf_op jit(solution)/shard_map/all_gather | solution.py:165
  78.9 38.5 %shard_map.49 = (f32[1536,1]{1,0:T(8,128)}, f32[1536,1]{1,0:T(8,128)}, f32[1536,256]{1,0:T(8,128)}, f32[1536,1]{1,0:T(8,128)}, f32[1536,1]{1,0:T(8,128)}) custom-call(bf16[1536,256]{1,0:T(8,128)(2,1)} %all_gather.9.q_ref, bf16[6144,256]{1,0:T(8,128)(2,1)} %bitcast.61, f32[1,6144]{1,0:T(1,128)} %sub.117.y_ref, f32[1,6144]{1,0:T(1,128)} %reshape.360.x_ref), custom_call_target="tpu_custom_call" | custom-call | tf_op jit(solution)/shard_map/pallas_call | solution.py:116
  117.4 1.6 reduce.1
  119.0 0.1 stack.38
  119.1 1.4 reduce.2
  120.5 0.1 stack.39
  120.6 0.3 reduce.3
  120.9 0.1 stack.40
  120.9 0.3 reduce.4
  121.2 0.1 stack.41
  121.3 1.3 select_maximum_fusion
  122.7 4.8 %all-to-all-start = ((f32[8,196,256]{2,1,0:T(8,128)}), f32[8,196,256]{2,1,0:T(8,128)S(1)}, u32[]{:S(2)}, u32[]{:S(2)}) async-start(f32[8,196,256]{2,1,0:T(8,128)} %select_maximum_fusion), calls=%async_computation | async-start | bytes 3276800 | tf_op jit(solution)/shard_map/all_to_all | solution.py:196
  127.5 20.1 %all-to-all-done = f32[8,196,256]{2,1,0:T(8,128)S(1)} async-done(((f32[8,196,256]{2,1,0:T(8,128)}), f32[8,196,256]{2,1,0:T(8,128)S(1)}, u32[]{:S(2)}, u32[]{:S(2)}) %all-to-all-start) | async-done | bytes 1605664 | tf_op jit(solution)/shard_map/all_to_all | solution.py:196
  147.7 0.1 div.142
  147.8 0.1 div.139
  147.9 0.1 div.141
  148.0 0.1 broadcast_subtract_fusion
  148.1 1.9 collective-permute-start.4
  150.0 2.4 %collective-permute-start.5 = (f32[2,1,48]{2,1,0:T(1,128)S(1)}, f32[2,1,48]{2,1,0:T(1,128)S(1)}, u32[]{:S(2)}, u32[]{:S(2)}) collective-permute-start(f32[2,1,48]{2,1,0:T(1,128)S(1)} %get-tuple-element.47), channel_id=1, source_target_pairs={{0,8},{8,16},{16,24},{24,32},{32,40},{40,48},{48,56},{56,64},{64,7... | collective-permute-start | bytes 1160 | tf_op jit(solution)/shard_map/ppermute | solution.py:31
  152.4 0.3 fusion
  152.7 0.1 divide_convert_fusion.1
  152.8 0.6 pad_maximum_fusion.16
  153.4 2.7 %collective-permute-start = (bf16[2,1,48,256]{3,2,1,0:T(8,128)(2,1)S(1)}, bf16[2,1,48,256]{3,2,1,0:T(8,128)(2,1)S(1)}, u32[]{:S(2)}, u32[]{:S(2)}) collective-permute-start(bf16[2,1,48,256]{3,2,1,0:T(8,128)(2,1)S(1)} %get-tuple-element.43), channel_id=1, source_target_pairs={{0,8},{8,16},{16,24},{24,32},{32,40},{40,48},{48,56},{56,64},{64,7... | collective-permute-start | bytes 147464 | tf_op jit(solution)/shard_map/ppermute | solution.py:31
  156.1 5.0 %collective-permute-start.1 = (bf16[2,1,48,256]{3,2,1,0:T(8,128)(2,1)S(1)}, bf16[2,1,48,256]{3,2,1,0:T(8,128)(2,1)S(1)}, u32[]{:S(2)}, u32[]{:S(2)}) collective-permute-start(bf16[2,1,48,256]{3,2,1,0:T(8,128)(2,1)S(1)} %get-tuple-element.44), channel_id=1, source_target_pairs={{8,0},{16,8},{24,16},{32,24},{40,32},{48,40},{56,48},{64,56},{72,6... | collective-permute-start | bytes 147464 | tf_op jit(solution)/shard_map/ppermute | solution.py:32
  161.1 0.0 collective-permute-done.4
  161.1 0.0 collective-permute-done.5
  161.1 0.0 collective-permute-done
  161.1 1.7 collective-permute-done.1
  162.8 5.3 %collective-permute-start.2 = (bf16[2,6,1,256]{3,2,1,0:T(2,128)(2,1)S(1)}, bf16[2,6,1,256]{3,2,1,0:T(2,128)(2,1)S(1)}, u32[]{:S(2)}, u32[]{:S(2)}) collective-permute-start(bf16[2,6,1,256]{3,2,1,0:T(2,128)(2,1)S(1)} %get-tuple-element.41), channel_id=1, source_target_pairs={{0,1},{1,2},{2,3},{3,4},{4,5},{5,6},{6,7},{8,9},{9,10},{10,11},{11... | collective-permute-start | bytes 18440 | tf_op jit(solution)/shard_map/ppermute | solution.py:31
  168.2 1.9 collective-permute-start.3
  170.1 0.1 fusion.58
  170.2 1.9 collective-permute-start.6
  172.1 7.5 %collective-permute-start.7 = (f32[2,6,1]{2,1,0:T(8,128)S(1)}, f32[2,6,1]{2,1,0:T(8,128)S(1)}, u32[]{:S(2)}, u32[]{:S(2)}) collective-permute-start(f32[2,6,1]{2,1,0:T(8,128)S(1)} %get-tuple-element.46), channel_id=1, source_target_pairs={{0,1},{1,2},{2,3},{3,4},{4,5},{5,6},{6,7},{8,9},{9,10},{10,11},{11... | collective-permute-start | bytes 152 | tf_op jit(solution)/shard_map/ppermute | solution.py:31
  179.6 0.0 collective-permute-done.3
  179.6 0.1 pad_maximum_fusion
  179.8 0.1 fusion.30
  179.9 0.1 fusion.27
  179.9 0.1 fusion.2
  180.0 0.1 fusion.4
  180.2 0.8 fusion.34
  180.9 0.1 convert_bitcast_fusion
  181.1 1.9 collective-permute-start.8
  183.0 5.8 %collective-permute-start.9 = (bf16[3,1,48,256]{3,2,1,0:T(8,128)(2,1)S(1)}, bf16[3,1,48,256]{3,2,1,0:T(8,128)(2,1)S(1)}, u32[]{:S(2)}, u32[]{:S(2)}) collective-permute-start(bf16[3,1,48,256]{3,2,1,0:T(8,128)(2,1)S(1)} %get-tuple-element.40), channel_id=1, source_target_pairs={{8,0},{16,8},{24,16},{32,24},{40,32},{48,40},{56,48},{64,56},{72,6... | collective-permute-start | bytes 221192 | tf_op jit(solution)/shard_map/ppermute | solution.py:32
  188.8 0.1 multiply_select_fusion
  188.9 0.0 collective-permute-done.6
  188.9 0.0 collective-permute-done.7
  188.9 0.1 multiply_select_fusion.1
  189.0 1.8 collective-permute-done.9
  190.8 3.9 %collective-permute-start.10 = (bf16[3,6,1,256]{3,2,1,0:T(2,128)(2,1)S(1)}, bf16[3,6,1,256]{3,2,1,0:T(2,128)(2,1)S(1)}, u32[]{:S(2)}, u32[]{:S(2)}) collective-permute-start(bf16[3,6,1,256]{3,2,1,0:T(2,128)(2,1)S(1)} %get-tuple-element.32), channel_id=1, source_target_pairs={{0,1},{1,2},{2,3},{3,4},{4,5},{5,6},{6,7},{8,9},{9,10},{10,11},{11... | collective-permute-start | bytes 27656 | tf_op jit(solution)/shard_map/ppermute | solution.py:31
  194.7 1.9 collective-permute-start.11
  196.7 0.7 slice_subtract_fusion.2
  197.3 0.0 collective-permute-done.10
  197.3 6.7 %collective-permute-done.11 = bf16[3,6,1,256]{3,2,1,0:T(2,128)(2,1)S(1)} collective-permute-done((bf16[3,6,1,256]{3,2,1,0:T(2,128)(2,1)S(1)}, bf16[3,6,1,256]{3,2,1,0:T(2,128)(2,1)S(1)}, u32[]{:S(2)}, u32[]{:S(2)}) %collective-permute-start.11) | collective-permute-done | bytes 9248 | tf_op jit(solution)/shard_map/ppermute | solution.py:32
  204.0 0.1 maximum_convert_fusion
  204.1 0.1 slice_bitcast_fusion.2
  204.2 1.0 fusion.7
  (29 shorter events, 0.3 us)
Async XLA Ops:
  7.2 30.1 %copy-start = (bf16[4,48,256]{2,1,0:T(8,128)(2,1)S(1)}, bf16[4,48,256]{2,1,0:T(8,128)(2,1)}, u32[]{:S(2)}) copy-start(bf16[4,48,256]{2,1,0:T(8,128)(2,1)} %param.2) | copy-start | bytes 294916
  7.2 71.8 %all-gather.2.cloned.1.call-start = ((), (), s32[]{:S(2)}) async-start(), calls=%async_computation.1 | async-start | bytes 3932160 | tf_op jit(solution)/shard_map/all_gather | solution.py:165
  117.4 3.1 %copy-start.3 = (f32[1536,1]{1,0:T(8,128)S(1)}, f32[1536,1]{1,0:T(8,128)}, u32[]{:S(2)}) copy-start(f32[1536,1]{1,0:T(8,128)} %get-tuple-element.11) | copy-start | bytes 18436
  117.4 3.5 %copy-start.2 = (f32[1536,1]{1,0:T(8,128)S(1)}, f32[1536,1]{1,0:T(8,128)}, u32[]{:S(2)}) copy-start(f32[1536,1]{1,0:T(8,128)} %get-tuple-element.12) | copy-start | bytes 18436
  117.4 3.9 %copy-start.1 = (f32[1536,256]{1,0:T(8,128)S(1)}, f32[1536,256]{1,0:T(8,128)}, u32[]{:S(2)}) copy-start(f32[1536,256]{1,0:T(8,128)} %get-tuple-element.8) | copy-start | bytes 4718596
  122.7 25.0 %all-to-all-start = ((f32[8,196,256]{2,1,0:T(8,128)}), f32[8,196,256]{2,1,0:T(8,128)S(1)}, u32[]{:S(2)}, u32[]{:S(2)}) async-start(f32[8,196,256]{2,1,0:T(8,128)} %select_maximum_fusion), calls=%async_computation | async-start | bytes 3276800 | tf_op jit(solution)/shard_map/all_to_all | solution.py:196
  148.1 13.0 %collective-permute-start.4 = (f32[2,1,48]{2,1,0:T(1,128)S(1)}, f32[2,1,48]{2,1,0:T(1,128)S(1)}, u32[]{:S(2)}, u32[]{:S(2)}) collective-permute-start(f32[2,1,48]{2,1,0:T(1,128)S(1)} %get-tuple-element.48), channel_id=1, source_target_pairs={{8,0},{16,8},{24,16},{32,24},{40,32},{48,40},{56,48},{64,56},{72,6... | collective-permute-start | bytes 1160 | tf_op jit(solution)/shard_map/ppermute | solution.py:32
  150.0 11.1 %collective-permute-start.5 = (f32[2,1,48]{2,1,0:T(1,128)S(1)}, f32[2,1,48]{2,1,0:T(1,128)S(1)}, u32[]{:S(2)}, u32[]{:S(2)}) collective-permute-start(f32[2,1,48]{2,1,0:T(1,128)S(1)} %get-tuple-element.47), channel_id=1, source_target_pairs={{0,8},{8,16},{16,24},{24,32},{32,40},{40,48},{48,56},{56,64},{64,7... | collective-permute-start | bytes 1160 | tf_op jit(solution)/shard_map/ppermute | solution.py:31
  153.4 7.7 %collective-permute-start = (bf16[2,1,48,256]{3,2,1,0:T(8,128)(2,1)S(1)}, bf16[2,1,48,256]{3,2,1,0:T(8,128)(2,1)S(1)}, u32[]{:S(2)}, u32[]{:S(2)}) collective-permute-start(bf16[2,1,48,256]{3,2,1,0:T(8,128)(2,1)S(1)} %get-tuple-element.43), channel_id=1, source_target_pairs={{0,8},{8,16},{16,24},{24,32},{32,40},{40,48},{48,56},{56,64},{64,7... | collective-permute-start | bytes 147464 | tf_op jit(solution)/shard_map/ppermute | solution.py:31
  156.1 6.7 %collective-permute-start.1 = (bf16[2,1,48,256]{3,2,1,0:T(8,128)(2,1)S(1)}, bf16[2,1,48,256]{3,2,1,0:T(8,128)(2,1)S(1)}, u32[]{:S(2)}, u32[]{:S(2)}) collective-permute-start(bf16[2,1,48,256]{3,2,1,0:T(8,128)(2,1)S(1)} %get-tuple-element.44), channel_id=1, source_target_pairs={{8,0},{16,8},{24,16},{32,24},{40,32},{48,40},{56,48},{64,56},{72,6... | collective-permute-start | bytes 147464 | tf_op jit(solution)/shard_map/ppermute | solution.py:32
  162.8 16.8 %collective-permute-start.2 = (bf16[2,6,1,256]{3,2,1,0:T(2,128)(2,1)S(1)}, bf16[2,6,1,256]{3,2,1,0:T(2,128)(2,1)S(1)}, u32[]{:S(2)}, u32[]{:S(2)}) collective-permute-start(bf16[2,6,1,256]{3,2,1,0:T(2,128)(2,1)S(1)} %get-tuple-element.41), channel_id=1, source_target_pairs={{0,1},{1,2},{2,3},{3,4},{4,5},{5,6},{6,7},{8,9},{9,10},{10,11},{11... | collective-permute-start | bytes 18440 | tf_op jit(solution)/shard_map/ppermute | solution.py:31
  168.2 11.5 %collective-permute-start.3 = (bf16[2,6,1,256]{3,2,1,0:T(2,128)(2,1)S(1)}, bf16[2,6,1,256]{3,2,1,0:T(2,128)(2,1)S(1)}, u32[]{:S(2)}, u32[]{:S(2)}) collective-permute-start(bf16[2,6,1,256]{3,2,1,0:T(2,128)(2,1)S(1)} %get-tuple-element.42), channel_id=1, source_target_pairs={{1,0},{2,1},{3,2},{4,3},{5,4},{6,5},{7,6},{9,8},{10,9},{11,10},{12... | collective-permute-start | bytes 18440 | tf_op jit(solution)/shard_map/ppermute | solution.py:32
  170.2 18.7 %collective-permute-start.6 = (f32[2,6,1]{2,1,0:T(8,128)S(1)}, f32[2,6,1]{2,1,0:T(8,128)S(1)}, u32[]{:S(2)}, u32[]{:S(2)}) collective-permute-start(f32[2,6,1]{2,1,0:T(8,128)S(1)} %get-tuple-element.45), channel_id=1, source_target_pairs={{1,0},{2,1},{3,2},{4,3},{5,4},{6,5},{7,6},{9,8},{10,9},{11,10},{12... | collective-permute-start | bytes 152 | tf_op jit(solution)/shard_map/ppermute | solution.py:32
  172.1 16.8 %collective-permute-start.7 = (f32[2,6,1]{2,1,0:T(8,128)S(1)}, f32[2,6,1]{2,1,0:T(8,128)S(1)}, u32[]{:S(2)}, u32[]{:S(2)}) collective-permute-start(f32[2,6,1]{2,1,0:T(8,128)S(1)} %get-tuple-element.46), channel_id=1, source_target_pairs={{0,1},{1,2},{2,3},{3,4},{4,5},{5,6},{6,7},{8,9},{9,10},{10,11},{11... | collective-permute-start | bytes 152 | tf_op jit(solution)/shard_map/ppermute | solution.py:31
  181.1 7.9 %collective-permute-start.8 = (bf16[3,1,48,256]{3,2,1,0:T(8,128)(2,1)S(1)}, bf16[3,1,48,256]{3,2,1,0:T(8,128)(2,1)S(1)}, u32[]{:S(2)}, u32[]{:S(2)}) collective-permute-start(bf16[3,1,48,256]{3,2,1,0:T(8,128)(2,1)S(1)} %get-tuple-element.39), channel_id=1, source_target_pairs={{0,8},{8,16},{16,24},{24,32},{32,40},{40,48},{48,56},{56,64},{64,7... | collective-permute-start | bytes 221192 | tf_op jit(solution)/shard_map/ppermute | solution.py:31
  183.0 7.7 %collective-permute-start.9 = (bf16[3,1,48,256]{3,2,1,0:T(8,128)(2,1)S(1)}, bf16[3,1,48,256]{3,2,1,0:T(8,128)(2,1)S(1)}, u32[]{:S(2)}, u32[]{:S(2)}) collective-permute-start(bf16[3,1,48,256]{3,2,1,0:T(8,128)(2,1)S(1)} %get-tuple-element.40), channel_id=1, source_target_pairs={{8,0},{16,8},{24,16},{32,24},{40,32},{48,40},{56,48},{64,56},{72,6... | collective-permute-start | bytes 221192 | tf_op jit(solution)/shard_map/ppermute | solution.py:32
  190.8 6.5 %collective-permute-start.10 = (bf16[3,6,1,256]{3,2,1,0:T(2,128)(2,1)S(1)}, bf16[3,6,1,256]{3,2,1,0:T(2,128)(2,1)S(1)}, u32[]{:S(2)}, u32[]{:S(2)}) collective-permute-start(bf16[3,6,1,256]{3,2,1,0:T(2,128)(2,1)S(1)} %get-tuple-element.32), channel_id=1, source_target_pairs={{0,1},{1,2},{2,3},{3,4},{4,5},{5,6},{6,7},{8,9},{9,10},{10,11},{11... | collective-permute-start | bytes 27656 | tf_op jit(solution)/shard_map/ppermute | solution.py:31
  194.7 9.3 %collective-permute-start.11 = (bf16[3,6,1,256]{3,2,1,0:T(2,128)(2,1)S(1)}, bf16[3,6,1,256]{3,2,1,0:T(2,128)(2,1)S(1)}, u32[]{:S(2)}, u32[]{:S(2)}) collective-permute-start(bf16[3,6,1,256]{3,2,1,0:T(2,128)(2,1)S(1)} %get-tuple-element.33), channel_id=1, source_target_pairs={{1,0},{2,1},{3,2},{4,3},{5,4},{6,5},{7,6},{9,8},{10,9},{11,10},{12... | collective-permute-start | bytes 27656 | tf_op jit(solution)/shard_map/ppermute | solution.py:32
Sparse Core Ops, SparseCore 0:
  35.6 43.2 all-gather.1

commit v5 on v4

--- a/solution.py
+++ b/solution.py
@@ -210,23 +210,21 @@
             (along_x / total).reshape(rows, cols) - own_x[None, :],
         ]
     )
-    pair = jnp.stack([feat1, warped])
     xval = feat1.astype(jnp.float32)
     yval = warped.astype(jnp.float32)
-    margin = 1
-    padded = with_halo(pair, ((BLK, 1), (COL, 2)), 1)
-    xpad = padded[0].astype(jnp.float32)
-    ypad = padded[1].astype(jnp.float32)
+    margin = 2
+    xpad = with_halo(feat1, ((BLK, 0), (COL, 1)), margin).astype(jnp.float32)
+    ypad = with_halo(warped, ((BLK, 0), (COL, 1)), margin).astype(jnp.float32)
+    flow_pad = with_halo(flow, ((BLK, 1), (COL, 2)), 1)
     first, grad_var, grad_cov = local_terms(xpad, ypad)
-    maps = jnp.stack([first, grad_var, grad_cov])
-    beside_all = with_halo(maps.astype(jnp.bfloat16), ((BLK, 1), (COL, 2)), 1).astype(
-        maps.dtype
-    )
-    spread_first = box_valid(beside_all[0])
-    spread_var = box_valid(beside_all[1])
-    spread_cov = box_valid(beside_all[2])
+    cell_y = row_start - 1 + jnp.arange(rows + 2, dtype=jnp.int32)
+    cell_x = col_start - 1 + jnp.arange(cols + 2, dtype=jnp.int32)
+    inside = ((cell_y >= 0) & (cell_y < full_rows))[:, None] & ((cell_x >= 0) & (cell_x < full_cols))[None, :]
+    inside = inside[:, :, None]
+    spread_first = box_valid(jnp.where(inside, first, 0.0))
+    spread_var = box_valid(jnp.where(inside, grad_var, 0.0))
+    spread_cov = box_valid(jnp.where(inside, grad_cov, 0.0))
     grad_warped = spread_first + 2.0 * yval * spread_var + xval * spread_cov
-    flow_pad = with_halo(flow, ((BLK, 1), (COL, 2)), 1)
     x_rows = xpad[margin - 1 : margin + rows + 1, margin : margin + cols]
     x_cols = xpad[margin : margin + rows, margin - 1 : margin + cols + 1]
     edge_y = row_start - 1 + jnp.arange(rows + 1, dtype=jnp.int32)

time: 214 us -> 205 us (0.958)
  waiting for transfers between devices: 57.6 us -> 45.8 us
  starting transfers between devices: 47 us -> 49.5 us
    all_to_all x1, waiting for transfers between devices: 20.1 us -> 0.16 us  [body(): packed = lax.all_to_all(packed, QUERY_AXES, 0, 0, tiled=True)]
    ppermute x6, waiting for transfers between devices: 0.02 us -> 19.6 us  [with_halo(): before = lax.ppermute(last, axis, up)]
    all_gather x1, waiting for transfers between devices: 27.3 us -> 19.4 us  [body(): piece = lax.all_gather(piece, axis, axis=0, tiled=True)]
    ppermute x6, waiting for transfers between devices: 10.1 us -> 6.57 us  [with_halo(): after = lax.ppermute(first, axis, down)]
    ppermute x6, starting transfers between devices: 18.4 us -> 20.8 us  [with_halo(): after = lax.ppermute(first, axis, down)]
    select_n x0 -> x2, other arithmetic: none -> 2.18 us  [the longest x1 1.91 us: body(): spread_first = box_valid(jnp.where(inside, first, 0.0))]
  transfers between devices with their start and end apart: 14 -> 14, of which waited for: 5 -> 6; matrix products, arithmetic and copies ran while one was open for 2% -> 4% of each run, Pallas kernels for 0% -> 19%
where the time goes in v5:
time: 205 us; the launch traced here: 204 us
  starting transfers between devices  49.5 us (24%)
  waiting for transfers between devices  45.8 us (22%)
  blocking collectives  42.7 us (21%)
  Pallas kernels  38.5 us (19%)
  between operations  14.4 us (7%)
  other arithmetic  11 us (5%)
  local copies, waits for them, and re-layouts  2.22 us (1%)
    pallas_call x1, Pallas kernels, flash_partials(): pl.pallas_call(kernel, grid=grid, in_specs=[pl.BlockSpec((block_q, width)...  38.5 us
    all_gather x1, blocking collectives, body(): piece = lax.all_gather(piece, axis, axis=0, tiled=True)  28.3 us
    ppermute x6, starting transfers between devices, with_halo(): before = lax.ppermute(last, axis, up)  23.8 us
    ppermute x6, starting transfers between devices, with_halo(): after = lax.ppermute(first, axis, down)  20.8 us
    ppermute x6, waiting for transfers between devices, with_halo(): before = lax.ppermute(last, axis, up)  19.6 us
    all_gather x1, waiting for transfers between devices, body(): piece = lax.all_gather(piece, axis, axis=0, tiled=True)  19.4 us
    all_gather x1, blocking collectives, body(): lax.all_gather(feat1.reshape(tokens, width), QUERY_AXES, axis=0, tiled=True)  14.4 us
    ppermute x6, waiting for transfers between devices, with_halo(): after = lax.ppermute(first, axis, down)  6.57 us
  transfers between devices with their start and end apart: 14, of which 6 were waited for; matrix products, arithmetic and copies ran while one was open for 4% of the time, Pallas kernels for 19%

profile of v5, /device:TPU:152, one launch (start us, length us, event | category | flops | bytes accessed | tf_op | source)
XLA Modules:
  0.0 204.1 jit_solution(12455311566124607983)
XLA Ops:
  7.2 0.0 all-gather.2.cloned.1.call-start
  7.2 28.3 %all_gather.10 = bf16[32,48,256]{2,1,0:T(8,128)(2,1)} all-gather(bf16[4,48,256]{2,1,0:T(8,128)(2,1)} %param.3), channel_id=1, replica_groups=mesh['z'=8,'xl'=2,'c'=2,'xh'=2,'y'=4] {'z'}, dimensions={0}, use_global_device_ids=true | all-gather | bytes 884736 | tf_op jit(solution)/shard_map/all_gather | solution.py:165
  35.5 0.0 all-gather.2.cloned.1.call-update
  35.6 1.9 collective-permute-start
  37.5 5.8 %collective-permute-start.1 = (bf16[2,48,256]{2,1,0:T(8,128)(2,1)S(1)}, bf16[2,48,256]{2,1,0:T(8,128)(2,1)S(1)}, u32[]{:S(2)}, u32[]{:S(2)}) collective-permute-start(bf16[2,48,256]{2,1,0:T(8,128)(2,1)S(1)} %get-tuple-element.38), channel_id=1, source_target_pairs={{8,0},{16,8},{24,16},{32,24},{40,32},{48,40},{56,48},{64,56},{72,6... | collective-permute-start | bytes 147464 | tf_op jit(solution)/shard_map/ppermute | solution.py:32
  43.3 0.1 broadcast_in_dim.67
  43.4 0.7 sub.119.y_ref
  44.1 0.1 multiply_add_fusion.2
  44.2 0.7 reshape.379.x_ref
  45.0 0.1 broadcast_and_fusion
  45.0 14.4 %all_gather.9.q_ref = bf16[1536,256]{1,0:T(8,128)(2,1)} all-gather(bf16[192,256]{1,0:T(8,128)(2,1)S(1)} %bitcast.35), channel_id=1, replica_groups=mesh['z'=8,'xl'=2,'c'=2,'xh'=2,'y'=4] {'y','c'}, dimensions={0}, use_global_device_ids=true | all-gather | bytes 884736 | tf_op jit(solution)/shard_map/all_gather | solution.py:155
  59.5 19.4 %all-gather.2.cloned.1.call-done = bf16[128,48,256]{2,1,0:T(8,128)(2,1)} async-done(((bf16[32,48,256]{2,1,0:T(8,128)(2,1)}), bf16[128,48,256]{2,1,0:T(8,128)(2,1)}) %all-gather.2.cloned.1.call-update) | async-done | bytes 3145744 | tf_op jit(solution)/shard_map/all_gather | solution.py:165
  78.9 38.5 %shard_map.49 = (f32[1536,1]{1,0:T(8,128)}, f32[1536,1]{1,0:T(8,128)}, f32[1536,256]{1,0:T(8,128)}, f32[1536,1]{1,0:T(8,128)}, f32[1536,1]{1,0:T(8,128)}) custom-call(bf16[1536,256]{1,0:T(8,128)(2,1)} %all_gather.9.q_ref, bf16[6144,256]{1,0:T(8,128)(2,1)} %bitcast.31, f32[1,6144]{1,0:T(1,128)} %sub.119.y_ref, f32[1,6144]{1,0:T(1,128)} %reshape.379.x_ref), custom_call_target="tpu_custom_call" | custom-call | tf_op jit(solution)/shard_map/pallas_call | solution.py:116
  117.5 1.6 reduce.1
  119.0 0.1 stack.16
  119.1 1.4 reduce.2
  120.5 0.1 stack.17
  120.6 0.3 reduce.3
  120.9 0.1 stack.18
  120.9 0.3 reduce.4
  121.2 0.1 stack.19
  121.3 1.3 select_maximum_fusion
  122.7 4.8 %all-to-all-start = ((f32[8,196,256]{2,1,0:T(8,128)}), f32[8,196,256]{2,1,0:T(8,128)S(1)}, u32[]{:S(2)}, u32[]{:S(2)}) async-start(f32[8,196,256]{2,1,0:T(8,128)} %select_maximum_fusion), calls=%async_computation | async-start | bytes 3276800 | tf_op jit(solution)/shard_map/all_to_all | solution.py:196
  127.5 0.0 collective-permute-done
  127.5 3.3 %collective-permute-start.2 = (bf16[8,2,256]{2,1,0:T(2,128)(2,1)S(1)}, bf16[8,2,256]{2,1,0:T(2,128)(2,1)S(1)}, u32[]{:S(2)}, u32[]{:S(2)}) collective-permute-start(bf16[8,2,256]{2,1,0:T(2,128)(2,1)S(1)} %get-tuple-element.34), channel_id=1, source_target_pairs={{0,1},{1,2},{2,3},{3,4},{4,5},{5,6},{6,7},{8,9},{9,10},{10,11},{11... | collective-permute-start | bytes 24584 | tf_op jit(solution)/shard_map/ppermute | solution.py:31
  130.8 2.6 %collective-permute-start.3 = (bf16[8,2,256]{2,1,0:T(2,128)(2,1)S(1)}, bf16[8,2,256]{2,1,0:T(2,128)(2,1)S(1)}, u32[]{:S(2)}, u32[]{:S(2)}) collective-permute-start(bf16[8,2,256]{2,1,0:T(2,128)(2,1)S(1)} %get-tuple-element.35), channel_id=1, source_target_pairs={{1,0},{2,1},{3,2},{4,3},{5,4},{6,5},{7,6},{9,8},{10,9},{11,10},{12... | collective-permute-start | bytes 24584 | tf_op jit(solution)/shard_map/ppermute | solution.py:32
  133.4 13.8 %collective-permute-done.2 = bf16[8,2,256]{2,1,0:T(2,128)(2,1)S(1)} collective-permute-done((bf16[8,2,256]{2,1,0:T(2,128)(2,1)S(1)}, bf16[8,2,256]{2,1,0:T(2,128)(2,1)S(1)}, u32[]{:S(2)}, u32[]{:S(2)}) %collective-permute-start.2) | collective-permute-done | bytes 8224 | tf_op jit(solution)/shard_map/ppermute | solution.py:31
  147.2 0.0 collective-permute-done.3
  147.2 0.1 maximum_convert_fusion
  147.3 0.1 fusion.20
  147.4 0.1 fusion.18
  147.6 0.2 all-to-all-done
  147.8 0.1 div.143
  147.9 0.1 div.132
  148.0 0.1 div.134
  148.1 0.1 broadcast_subtract_fusion
  148.2 0.6 pad_maximum_fusion.4
  148.8 0.3 fusion
  149.0 0.1 divide_convert_fusion.1
  149.2 1.9 collective-permute-start.8
  151.1 5.8 %collective-permute-start.9 = (bf16[2,48,256]{2,1,0:T(8,128)(2,1)S(1)}, bf16[2,48,256]{2,1,0:T(8,128)(2,1)S(1)}, u32[]{:S(2)}, u32[]{:S(2)}) collective-permute-start(bf16[2,48,256]{2,1,0:T(8,128)(2,1)S(1)} %bitcast.36), channel_id=1, source_target_pairs={{8,0},{16,8},{24,16},{32,24},{40,32},{48,40},{56,48},{64,56},{72,6... | collective-permute-start | bytes 147464 | tf_op jit(solution)/shard_map/ppermute | solution.py:32
  156.8 1.9 collective-permute-start.4
  158.8 2.4 %collective-permute-start.5 = (f32[2,1,48]{2,1,0:T(1,128)S(1)}, f32[2,1,48]{2,1,0:T(1,128)S(1)}, u32[]{:S(2)}, u32[]{:S(2)}) collective-permute-start(f32[2,1,48]{2,1,0:T(1,128)S(1)} %get-tuple-element.42), channel_id=1, source_target_pairs={{0,8},{8,16},{16,24},{24,32},{32,40},{40,48},{48,56},{56,64},{64,7... | collective-permute-start | bytes 1160 | tf_op jit(solution)/shard_map/ppermute | solution.py:31
  161.2 0.1 divide_convert_fusion
  161.3 0.0 collective-permute-done.4
  161.3 4.5 %collective-permute-done.5 = f32[2,1,48]{2,1,0:T(1,128)S(1)} collective-permute-done((f32[2,1,48]{2,1,0:T(1,128)S(1)}, f32[2,1,48]{2,1,0:T(1,128)S(1)}, u32[]{:S(2)}, u32[]{:S(2)}) %collective-permute-start.5) | collective-permute-done | bytes 416 | tf_op jit(solution)/shard_map/ppermute | solution.py:31
  165.8 0.1 fusion.57
  165.9 2.9 %collective-permute-start.6 = (f32[2,6,1]{2,1,0:T(8,128)S(1)}, f32[2,6,1]{2,1,0:T(8,128)S(1)}, u32[]{:S(2)}, u32[]{:S(2)}) collective-permute-start(f32[2,6,1]{2,1,0:T(8,128)S(1)} %get-tuple-element.40), channel_id=1, source_target_pairs={{1,0},{2,1},{3,2},{4,3},{5,4},{6,5},{7,6},{9,8},{10,9},{11,10},{12... | collective-permute-start | bytes 152 | tf_op jit(solution)/shard_map/ppermute | solution.py:32
  168.8 6.5 %collective-permute-start.7 = (f32[2,6,1]{2,1,0:T(8,128)S(1)}, f32[2,6,1]{2,1,0:T(8,128)S(1)}, u32[]{:S(2)}, u32[]{:S(2)}) collective-permute-start(f32[2,6,1]{2,1,0:T(8,128)S(1)} %get-tuple-element.41), channel_id=1, source_target_pairs={{0,1},{1,2},{2,3},{3,4},{4,5},{5,6},{6,7},{8,9},{9,10},{10,11},{11... | collective-permute-start | bytes 152 | tf_op jit(solution)/shard_map/ppermute | solution.py:31
  175.3 0.1 multiply_select_fusion
  175.4 0.0 collective-permute-done.6
  175.4 1.3 collective-permute-done.7
  176.7 0.1 multiply_select_fusion.1
  176.8 0.0 collective-permute-done.8
  176.8 0.0 collective-permute-done.9
  176.8 7.8 %collective-permute-start.10 = (bf16[8,2,256]{2,1,0:T(2,128)(2,1)S(1)}, bf16[8,2,256]{2,1,0:T(2,128)(2,1)S(1)}, u32[]{:S(2)}, u32[]{:S(2)}) collective-permute-start(bf16[8,2,256]{2,1,0:T(2,128)(2,1)S(1)} %get-tuple-element.32), channel_id=1, source_target_pairs={{0,1},{1,2},{2,3},{3,4},{4,5},{5,6},{6,7},{8,9},{9,10},{10,11},{11... | collective-permute-start | bytes 24584 | tf_op jit(solution)/shard_map/ppermute | solution.py:31
  184.6 1.9 collective-permute-start.11
  186.5 0.7 slice_subtract_fusion.2
  187.2 6.6 %collective-permute-done.11 = bf16[8,2,256]{2,1,0:T(2,128)(2,1)S(1)} collective-permute-done((bf16[8,2,256]{2,1,0:T(2,128)(2,1)S(1)}, bf16[8,2,256]{2,1,0:T(2,128)(2,1)S(1)}, u32[]{:S(2)}, u32[]{:S(2)}) %collective-permute-start.11) | collective-permute-done | bytes 8224 | tf_op jit(solution)/shard_map/ppermute | solution.py:32
  193.8 0.1 maximum_convert_fusion.1
  193.8 0.2 fusion.46
  194.0 1.9 fusion.14
  195.9 0.3 broadcast_select_fusion
  196.2 1.0 fusion.23
  (34 shorter events, 0.3 us)
Async XLA Ops:
  7.2 28.4 %copy-start.1 = (bf16[4,48,256]{2,1,0:T(8,128)(2,1)S(1)}, bf16[4,48,256]{2,1,0:T(8,128)(2,1)}, u32[]{:S(2)}) copy-start(bf16[4,48,256]{2,1,0:T(8,128)(2,1)} %param.2) | copy-start | bytes 294916
  7.2 71.8 %all-gather.2.cloned.1.call-start = ((), (), s32[]{:S(2)}) async-start(), calls=%async_computation.1 | async-start | bytes 3932160 | tf_op jit(solution)/shard_map/all_gather | solution.py:165
  35.6 91.9 %collective-permute-start = (bf16[2,48,256]{2,1,0:T(8,128)(2,1)S(1)}, bf16[2,48,256]{2,1,0:T(8,128)(2,1)S(1)}, u32[]{:S(2)}, u32[]{:S(2)}) collective-permute-start(bf16[2,48,256]{2,1,0:T(8,128)(2,1)S(1)} %get-tuple-element.39), channel_id=1, source_target_pairs={{0,8},{8,16},{16,24},{24,32},{32,40},{40,48},{48,56},{56,64},{64,7... | collective-permute-start | bytes 147464 | tf_op jit(solution)/shard_map/ppermute | solution.py:31
  37.5 90.0 %collective-permute-start.1 = (bf16[2,48,256]{2,1,0:T(8,128)(2,1)S(1)}, bf16[2,48,256]{2,1,0:T(8,128)(2,1)S(1)}, u32[]{:S(2)}, u32[]{:S(2)}) collective-permute-start(bf16[2,48,256]{2,1,0:T(8,128)(2,1)S(1)} %get-tuple-element.38), channel_id=1, source_target_pairs={{8,0},{16,8},{24,16},{32,24},{40,32},{48,40},{56,48},{64,56},{72,6... | collective-permute-start | bytes 147464 | tf_op jit(solution)/shard_map/ppermute | solution.py:32
  117.4 3.1 %copy-start.3 = (f32[1536,1]{1,0:T(8,128)S(1)}, f32[1536,1]{1,0:T(8,128)}, u32[]{:S(2)}) copy-start(f32[1536,1]{1,0:T(8,128)} %get-tuple-element.11) | copy-start | bytes 18436
  117.5 3.5 %copy-start.2 = (f32[1536,1]{1,0:T(8,128)S(1)}, f32[1536,1]{1,0:T(8,128)}, u32[]{:S(2)}) copy-start(f32[1536,1]{1,0:T(8,128)} %get-tuple-element.12) | copy-start | bytes 18436
  117.5 3.9 %copy-start = (f32[1536,256]{1,0:T(8,128)S(1)}, f32[1536,256]{1,0:T(8,128)}, u32[]{:S(2)}) copy-start(f32[1536,256]{1,0:T(8,128)} %get-tuple-element.8) | copy-start | bytes 4718596
  122.7 25.1 %all-to-all-start = ((f32[8,196,256]{2,1,0:T(8,128)}), f32[8,196,256]{2,1,0:T(8,128)S(1)}, u32[]{:S(2)}, u32[]{:S(2)}) async-start(f32[8,196,256]{2,1,0:T(8,128)} %select_maximum_fusion), calls=%async_computation | async-start | bytes 3276800 | tf_op jit(solution)/shard_map/all_to_all | solution.py:196
  127.5 19.7 %collective-permute-start.2 = (bf16[8,2,256]{2,1,0:T(2,128)(2,1)S(1)}, bf16[8,2,256]{2,1,0:T(2,128)(2,1)S(1)}, u32[]{:S(2)}, u32[]{:S(2)}) collective-permute-start(bf16[8,2,256]{2,1,0:T(2,128)(2,1)S(1)} %get-tuple-element.34), channel_id=1, source_target_pairs={{0,1},{1,2},{2,3},{3,4},{4,5},{5,6},{6,7},{8,9},{9,10},{10,11},{11... | collective-permute-start | bytes 24584 | tf_op jit(solution)/shard_map/ppermute | solution.py:31
  130.8 16.4 %collective-permute-start.3 = (bf16[8,2,256]{2,1,0:T(2,128)(2,1)S(1)}, bf16[8,2,256]{2,1,0:T(2,128)(2,1)S(1)}, u32[]{:S(2)}, u32[]{:S(2)}) collective-permute-start(bf16[8,2,256]{2,1,0:T(2,128)(2,1)S(1)} %get-tuple-element.35), channel_id=1, source_target_pairs={{1,0},{2,1},{3,2},{4,3},{5,4},{6,5},{7,6},{9,8},{10,9},{11,10},{12... | collective-permute-start | bytes 24584 | tf_op jit(solution)/shard_map/ppermute | solution.py:32
  149.2 27.6 %collective-permute-start.8 = (bf16[2,48,256]{2,1,0:T(8,128)(2,1)S(1)}, bf16[2,48,256]{2,1,0:T(8,128)(2,1)S(1)}, u32[]{:S(2)}, u32[]{:S(2)}) collective-permute-start(bf16[2,48,256]{2,1,0:T(8,128)(2,1)S(1)} %bitcast.37), channel_id=1, source_target_pairs={{0,8},{8,16},{16,24},{24,32},{32,40},{40,48},{48,56},{56,64},{64,7... | collective-permute-start | bytes 147464 | tf_op jit(solution)/shard_map/ppermute | solution.py:31
  151.1 25.7 %collective-permute-start.9 = (bf16[2,48,256]{2,1,0:T(8,128)(2,1)S(1)}, bf16[2,48,256]{2,1,0:T(8,128)(2,1)S(1)}, u32[]{:S(2)}, u32[]{:S(2)}) collective-permute-start(bf16[2,48,256]{2,1,0:T(8,128)(2,1)S(1)} %bitcast.36), channel_id=1, source_target_pairs={{8,0},{16,8},{24,16},{32,24},{40,32},{48,40},{56,48},{64,56},{72,6... | collective-permute-start | bytes 147464 | tf_op jit(solution)/shard_map/ppermute | solution.py:32
  156.8 4.5 %collective-permute-start.4 = (f32[2,1,48]{2,1,0:T(1,128)S(1)}, f32[2,1,48]{2,1,0:T(1,128)S(1)}, u32[]{:S(2)}, u32[]{:S(2)}) collective-permute-start(f32[2,1,48]{2,1,0:T(1,128)S(1)} %get-tuple-element.43), channel_id=1, source_target_pairs={{8,0},{16,8},{24,16},{32,24},{40,32},{48,40},{56,48},{64,56},{72,6... | collective-permute-start | bytes 1160 | tf_op jit(solution)/shard_map/ppermute | solution.py:32
  158.8 7.0 %collective-permute-start.5 = (f32[2,1,48]{2,1,0:T(1,128)S(1)}, f32[2,1,48]{2,1,0:T(1,128)S(1)}, u32[]{:S(2)}, u32[]{:S(2)}) collective-permute-start(f32[2,1,48]{2,1,0:T(1,128)S(1)} %get-tuple-element.42), channel_id=1, source_target_pairs={{0,8},{8,16},{16,24},{24,32},{32,40},{40,48},{48,56},{56,64},{64,7... | collective-permute-start | bytes 1160 | tf_op jit(solution)/shard_map/ppermute | solution.py:31
  165.9 9.5 %collective-permute-start.6 = (f32[2,6,1]{2,1,0:T(8,128)S(1)}, f32[2,6,1]{2,1,0:T(8,128)S(1)}, u32[]{:S(2)}, u32[]{:S(2)}) collective-permute-start(f32[2,6,1]{2,1,0:T(8,128)S(1)} %get-tuple-element.40), channel_id=1, source_target_pairs={{1,0},{2,1},{3,2},{4,3},{5,4},{6,5},{7,6},{9,8},{10,9},{11,10},{12... | collective-permute-start | bytes 152 | tf_op jit(solution)/shard_map/ppermute | solution.py:32
  168.8 7.9 %collective-permute-start.7 = (f32[2,6,1]{2,1,0:T(8,128)S(1)}, f32[2,6,1]{2,1,0:T(8,128)S(1)}, u32[]{:S(2)}, u32[]{:S(2)}) collective-permute-start(f32[2,6,1]{2,1,0:T(8,128)S(1)} %get-tuple-element.41), channel_id=1, source_target_pairs={{0,1},{1,2},{2,3},{3,4},{4,5},{5,6},{6,7},{8,9},{9,10},{10,11},{11... | collective-permute-start | bytes 152 | tf_op jit(solution)/shard_map/ppermute | solution.py:31
  176.8 10.4 %collective-permute-start.10 = (bf16[8,2,256]{2,1,0:T(2,128)(2,1)S(1)}, bf16[8,2,256]{2,1,0:T(2,128)(2,1)S(1)}, u32[]{:S(2)}, u32[]{:S(2)}) collective-permute-start(bf16[8,2,256]{2,1,0:T(2,128)(2,1)S(1)} %get-tuple-element.32), channel_id=1, source_target_pairs={{0,1},{1,2},{2,3},{3,4},{4,5},{5,6},{6,7},{8,9},{9,10},{10,11},{11... | collective-permute-start | bytes 24584 | tf_op jit(solution)/shard_map/ppermute | solution.py:31
  184.6 9.2 %collective-permute-start.11 = (bf16[8,2,256]{2,1,0:T(2,128)(2,1)S(1)}, bf16[8,2,256]{2,1,0:T(2,128)(2,1)S(1)}, u32[]{:S(2)}, u32[]{:S(2)}) collective-permute-start(bf16[8,2,256]{2,1,0:T(2,128)(2,1)S(1)} %get-tuple-element.33), channel_id=1, source_target_pairs={{1,0},{2,1},{3,2},{4,3},{5,4},{6,5},{7,6},{9,8},{10,9},{11,10},{12... | collective-permute-start | bytes 24584 | tf_op jit(solution)/shard_map/ppermute | solution.py:32
Sparse Core Ops, SparseCore 0:
  35.6 43.2 all-gather.1

commit v6 on v5

--- a/solution.py
+++ b/solution.py
@@ -15,7 +15,6 @@
 FINE = ("z", "xl", "c", "xh", "y")
 BLK = ("z", "xl", "c")
 COL = ("xh", "y")
-KEY_AXES = ("z", ("xh", "xl"))
 QUERY_AXES = ("y", "c")
 BLOCK_Q = 512
 BLOCK_K = 1024
@@ -160,20 +159,18 @@
     def norm_x(index):
         return (index.astype(jnp.float32) + 0.5) * (2.0 / full_cols) - 1.0
 
-    piece = feat2
-    for axis in KEY_AXES:
-        piece = lax.all_gather(piece, axis, axis=0, tiled=True)
+    sz, sxl, sc, sxh, sy = (lax.axis_size(a) for a in FINE)
+    blocks = [feat2]
+    for shift in range(1, sz):
+        ring = [(i, (i + shift) % sz) for i in range(sz)]
+        blocks.append(lax.ppermute(feat2, "z", ring))
+    piece = lax.all_gather(jnp.concatenate(blocks, axis=0), ("xh", "xl"), axis=0, tiled=True)
     count = piece.shape[0]
     gathered = jnp.arange(count, dtype=jnp.int32)
     rest = gathered // rows
-    place = {}
-    for axis in KEY_AXES:
-        size = lax.axis_size(axis)
-        place[axis] = rest % size
-        rest = rest // size
-    sz, sxl, sc, sxh, sy = (lax.axis_size(a) for a in FINE)
-    x_full = place[("xh", "xl")]
-    blk_of = (place["z"] * sxl + x_full % sxl) * sc + lax.axis_index("c")
+    z_from = (lax.axis_index("z") - rest % sz) % sz
+    x_full = rest // sz
+    blk_of = (z_from * sxl + x_full % sxl) * sc + lax.axis_index("c")
     col_of = (x_full // sxl) * sy + lax.axis_index("y")
     tile_y = blk_of * rows + gathered % rows
     tile_x = col_of * cols

time: 205 us -> 203 us (level)
  blocking collectives: 42.7 us -> 14.4 us
  starting transfers between devices: 49.5 us -> 64.4 us
  waiting for transfers between devices: 45.8 us -> 55.4 us
    all_gather x1 -> x0, blocking collectives: 28.3 us -> none  [body(): piece = lax.all_gather(piece, axis, axis=0, tiled=True)]
    ppermute x0 -> x7, waiting for transfers between devices: none -> 13.2 us  [body(): blocks.append(lax.ppermute(feat2, 'z', ring))]
    ppermute x6, waiting for transfers between devices: 19.6 us -> 7.04 us  [with_halo(): before = lax.ppermute(last, axis, up)]
    ppermute x0 -> x7, starting transfers between devices: none -> 11.3 us  [body(): blocks.append(lax.ppermute(feat2, 'z', ring))]
    ppermute x6, waiting for transfers between devices: 6.57 us -> 15.5 us  [with_halo(): after = lax.ppermute(first, axis, down)]
    ppermute x6, starting transfers between devices: 23.8 us -> 27.3 us  [with_halo(): before = lax.ppermute(last, axis, up)]
  transfers between devices with their start and end apart: 14 -> 21, of which waited for: 6 -> 12; matrix products, arithmetic and copies ran while one was open for 4% -> 5% of each run, Pallas kernels for 19% -> 19%
where the time goes in v6:
time: 203 us; the launch traced here: 202 us
  starting transfers between devices  64.4 us (32%)
  waiting for transfers between devices  55.4 us (27%)
  Pallas kernels  38.5 us (19%)
  blocking collectives  14.4 us (7%)
  between operations  14.4 us (7%)
  other arithmetic  11 us (5%)
  local copies, waits for them, and re-layouts  4.11 us (2%)
    pallas_call x1, Pallas kernels, flash_partials(): pl.pallas_call(kernel, grid=grid, in_specs=[pl.BlockSpec((block_q, width)...  38.5 us
    ppermute x6, starting transfers between devices, with_halo(): before = lax.ppermute(last, axis, up)  27.3 us
    ppermute x6, starting transfers between devices, with_halo(): after = lax.ppermute(first, axis, down)  21 us
    all_gather x1, waiting for transfers between devices, body(): lax.all_gather(jnp.concatenate(blocks, axis=0), ('xh', 'xl'), axis=0, til...  19.4 us
    ppermute x6, waiting for transfers between devices, with_halo(): after = lax.ppermute(first, axis, down)  15.5 us
    all_gather x1, blocking collectives, body(): lax.all_gather(feat1.reshape(tokens, width), QUERY_AXES, axis=0, tiled=True)  14.4 us
    ppermute x7, waiting for transfers between devices, body(): blocks.append(lax.ppermute(feat2, 'z', ring))  13.2 us
    ppermute x7, starting transfers between devices, body(): blocks.append(lax.ppermute(feat2, 'z', ring))  11.3 us
  transfers between devices with their start and end apart: 21, of which 12 were waited for; matrix products, arithmetic and copies ran while one was open for 5% of the time, Pallas kernels for 19%

profile of v6, /device:TPU:152, one launch (start us, length us, event | category | flops | bytes accessed | tf_op | source)
XLA Modules:
  0.0 202.2 jit_solution(14706294945332825391)
XLA Ops:
  7.2 1.1 collective-permute-start
  8.3 1.5 collective-permute-start.1
  9.8 0.1 collective-permute-start.2
  9.9 5.4 %collective-permute-start.3 = (bf16[4,48,256]{2,1,0:T(8,128)(2,1)}, bf16[4,48,256]{2,1,0:T(8,128)(2,1)S(1)}, u32[]{:S(2)}, u32[]{:S(2)}) collective-permute-start(bf16[4,48,256]{2,1,0:T(8,128)(2,1)} %param.3), channel_id=1, source_target_pairs={{0,128},{32,160},{64,192},{96,224},{128,0},{160,32},{192,64},{224,... | collective-permute-start | bytes 294920 | tf_op jit(solution)/shard_map/ppermute | solution.py:166
  15.3 1.0 collective-permute-start.4
  16.3 0.9 constant_dynamic-update-slice_fusion.7
  17.2 2.2 %collective-permute-start.5 = (bf16[4,48,256]{2,1,0:T(8,128)(2,1)}, bf16[4,48,256]{2,1,0:T(8,128)(2,1)S(1)}, u32[]{:S(2)}, u32[]{:S(2)}) collective-permute-start(bf16[4,48,256]{2,1,0:T(8,128)(2,1)} %param.3), channel_id=1, source_target_pairs={{0,192},{32,224},{64,0},{96,32},{128,64},{160,96},{192,128},{224,1... | collective-permute-start | bytes 294920 | tf_op jit(solution)/shard_map/ppermute | solution.py:166
  19.4 2.7 %collective-permute-done.1 = bf16[4,48,256]{2,1,0:T(8,128)(2,1)S(1)} collective-permute-done((bf16[4,48,256]{2,1,0:T(8,128)(2,1)}, bf16[4,48,256]{2,1,0:T(8,128)(2,1)S(1)}, u32[]{:S(2)}, u32[]{:S(2)}) %collective-permute-start.1) | collective-permute-done | bytes 98336 | tf_op jit(solution)/shard_map/ppermute | solution.py:166
  22.2 2.7 %collective-permute-done.2 = bf16[4,48,256]{2,1,0:T(8,128)(2,1)S(1)} collective-permute-done((bf16[4,48,256]{2,1,0:T(8,128)(2,1)}, bf16[4,48,256]{2,1,0:T(8,128)(2,1)S(1)}, u32[]{:S(2)}, u32[]{:S(2)}) %collective-permute-start.2) | collective-permute-done | bytes 98336 | tf_op jit(solution)/shard_map/ppermute | solution.py:166
  24.8 1.1 collective-permute-done.4
  26.0 4.8 %collective-permute-done.5 = bf16[4,48,256]{2,1,0:T(8,128)(2,1)S(1)} collective-permute-done((bf16[4,48,256]{2,1,0:T(8,128)(2,1)}, bf16[4,48,256]{2,1,0:T(8,128)(2,1)S(1)}, u32[]{:S(2)}, u32[]{:S(2)}) %collective-permute-start.5) | collective-permute-done | bytes 98336 | tf_op jit(solution)/shard_map/ppermute | solution.py:166
  30.8 2.0 collective-permute-done.6
  32.7 0.9 copy-done.2
  33.7 1.9 collective-permute-start.7
  35.6 5.8 %collective-permute-start.8 = (bf16[2,48,256]{2,1,0:T(8,128)(2,1)S(1)}, bf16[2,48,256]{2,1,0:T(8,128)(2,1)S(1)}, u32[]{:S(2)}, u32[]{:S(2)}) collective-permute-start(bf16[2,48,256]{2,1,0:T(8,128)(2,1)S(1)} %get-tuple-element.38), channel_id=1, source_target_pairs={{8,0},{16,8},{24,16},{32,24},{40,32},{48,40},{56,48},{64,56},{72,6... | collective-permute-start | bytes 147464 | tf_op jit(solution)/shard_map/ppermute | solution.py:31
  41.4 0.1 broadcast_in_dim.67
  41.5 0.7 sub.133.y_ref
  42.2 0.1 multiply_add_fusion.2
  42.3 0.7 reshape.380.x_ref
  43.1 0.1 broadcast_and_fusion
  43.2 14.4 %all_gather.6.q_ref = bf16[1536,256]{1,0:T(8,128)(2,1)} all-gather(bf16[192,256]{1,0:T(8,128)(2,1)S(1)} %bitcast.35), channel_id=1, replica_groups=mesh['z'=8,'xl'=2,'c'=2,'xh'=2,'y'=4] {'y','c'}, dimensions={0}, use_global_device_ids=true | all-gather | bytes 884736 | tf_op jit(solution)/shard_map/all_gather | solution.py:154
  57.6 19.4 %all-gather.2.cloned.1.call-done = bf16[128,48,256]{2,1,0:T(8,128)(2,1)} async-done(((bf16[32,48,256]{2,1,0:T(8,128)(2,1)}), bf16[128,48,256]{2,1,0:T(8,128)(2,1)}) %all-gather.2.cloned.1.call-update) | async-done | bytes 3145744 | tf_op jit(solution)/shard_map/all_gather | solution.py:167
  77.1 38.5 %shard_map.49 = (f32[1536,1]{1,0:T(8,128)}, f32[1536,1]{1,0:T(8,128)}, f32[1536,256]{1,0:T(8,128)}, f32[1536,1]{1,0:T(8,128)}, f32[1536,1]{1,0:T(8,128)}) custom-call(bf16[1536,256]{1,0:T(8,128)(2,1)} %all_gather.6.q_ref, bf16[6144,256]{1,0:T(8,128)(2,1)} %bitcast.31, f32[1,6144]{1,0:T(1,128)} %sub.133.y_ref, f32[1,6144]{1,0:T(1,128)} %reshape.380.x_ref), custom_call_target="tpu_custom_call" | custom-call | tf_op jit(solution)/shard_map/pallas_call | solution.py:115
  115.6 1.6 reduce.1
  117.2 1.4 reduce.2
  118.7 0.3 reduce.3
  119.0 0.1 stack.18
  119.1 0.3 reduce.4
  119.4 0.1 stack.19
  119.5 1.4 select_maximum_fusion
  120.8 4.8 %all-to-all-start = ((f32[8,196,256]{2,1,0:T(8,128)}), f32[8,196,256]{2,1,0:T(8,128)S(1)}, u32[]{:S(2)}, u32[]{:S(2)}) async-start(f32[8,196,256]{2,1,0:T(8,128)} %select_maximum_fusion), calls=%async_computation | async-start | bytes 3276800 | tf_op jit(solution)/shard_map/all_to_all | solution.py:193
  125.7 2.8 %collective-permute-start.10 = (bf16[8,2,256]{2,1,0:T(2,128)(2,1)S(1)}, bf16[8,2,256]{2,1,0:T(2,128)(2,1)S(1)}, u32[]{:S(2)}, u32[]{:S(2)}) collective-permute-start(bf16[8,2,256]{2,1,0:T(2,128)(2,1)S(1)} %get-tuple-element.35), channel_id=1, source_target_pairs={{1,0},{2,1},{3,2},{4,3},{5,4},{6,5},{7,6},{9,8},{10,9},{11,10},{12... | collective-permute-start | bytes 24584 | tf_op jit(solution)/shard_map/ppermute | solution.py:31
  128.5 6.7 %collective-permute-start.9 = (bf16[8,2,256]{2,1,0:T(2,128)(2,1)S(1)}, bf16[8,2,256]{2,1,0:T(2,128)(2,1)S(1)}, u32[]{:S(2)}, u32[]{:S(2)}) collective-permute-start(bf16[8,2,256]{2,1,0:T(2,128)(2,1)S(1)} %get-tuple-element.34), channel_id=1, source_target_pairs={{0,1},{1,2},{2,3},{3,4},{4,5},{5,6},{6,7},{8,9},{9,10},{10,11},{11... | collective-permute-start | bytes 24584 | tf_op jit(solution)/shard_map/ppermute | solution.py:30
  135.2 8.9 %collective-permute-done.10 = bf16[8,2,256]{2,1,0:T(2,128)(2,1)S(1)} collective-permute-done((bf16[8,2,256]{2,1,0:T(2,128)(2,1)S(1)}, bf16[8,2,256]{2,1,0:T(2,128)(2,1)S(1)}, u32[]{:S(2)}, u32[]{:S(2)}) %collective-permute-start.10) | collective-permute-done | bytes 8224 | tf_op jit(solution)/shard_map/ppermute | solution.py:31
  144.1 1.3 collective-permute-done.9
  145.4 0.1 fusion.20
  145.6 0.1 fusion.18
  145.7 0.2 all-to-all-done
  146.0 0.1 div.145
  146.1 0.1 div.134
  146.1 0.1 div.136
  146.2 0.1 broadcast_subtract_fusion
  146.3 0.6 pad_maximum_fusion.4
  146.9 0.3 fusion
  147.2 0.1 divide_convert_fusion.1
  147.3 1.9 collective-permute-start.15
  149.2 5.8 %collective-permute-start.16 = (bf16[2,48,256]{2,1,0:T(8,128)(2,1)S(1)}, bf16[2,48,256]{2,1,0:T(8,128)(2,1)S(1)}, u32[]{:S(2)}, u32[]{:S(2)}) collective-permute-start(bf16[2,48,256]{2,1,0:T(8,128)(2,1)S(1)} %bitcast.36), channel_id=1, source_target_pairs={{8,0},{16,8},{24,16},{32,24},{40,32},{48,40},{56,48},{64,56},{72,6... | collective-permute-start | bytes 147464 | tf_op jit(solution)/shard_map/ppermute | solution.py:31
  155.0 1.9 collective-permute-start.11
  156.9 2.4 %collective-permute-start.12 = (f32[2,1,48]{2,1,0:T(1,128)S(1)}, f32[2,1,48]{2,1,0:T(1,128)S(1)}, u32[]{:S(2)}, u32[]{:S(2)}) collective-permute-start(f32[2,1,48]{2,1,0:T(1,128)S(1)} %get-tuple-element.42), channel_id=1, source_target_pairs={{0,8},{8,16},{16,24},{24,32},{32,40},{40,48},{48,56},{56,64},{64,7... | collective-permute-start | bytes 1160 | tf_op jit(solution)/shard_map/ppermute | solution.py:30
  159.3 0.1 divide_convert_fusion
  159.5 4.5 %collective-permute-done.12 = f32[2,1,48]{2,1,0:T(1,128)S(1)} collective-permute-done((f32[2,1,48]{2,1,0:T(1,128)S(1)}, f32[2,1,48]{2,1,0:T(1,128)S(1)}, u32[]{:S(2)}, u32[]{:S(2)}) %collective-permute-start.12) | collective-permute-done | bytes 416 | tf_op jit(solution)/shard_map/ppermute | solution.py:30
  163.9 0.1 fusion.58
  164.0 2.9 %collective-permute-start.13 = (f32[2,6,1]{2,1,0:T(8,128)S(1)}, f32[2,6,1]{2,1,0:T(8,128)S(1)}, u32[]{:S(2)}, u32[]{:S(2)}) collective-permute-start(f32[2,6,1]{2,1,0:T(8,128)S(1)} %get-tuple-element.40), channel_id=1, source_target_pairs={{1,0},{2,1},{3,2},{4,3},{5,4},{6,5},{7,6},{9,8},{10,9},{11,10},{12... | collective-permute-start | bytes 152 | tf_op jit(solution)/shard_map/ppermute | solution.py:31
  166.9 6.5 %collective-permute-start.14 = (f32[2,6,1]{2,1,0:T(8,128)S(1)}, f32[2,6,1]{2,1,0:T(8,128)S(1)}, u32[]{:S(2)}, u32[]{:S(2)}) collective-permute-start(f32[2,6,1]{2,1,0:T(8,128)S(1)} %get-tuple-element.41), channel_id=1, source_target_pairs={{0,1},{1,2},{2,3},{3,4},{4,5},{5,6},{6,7},{8,9},{9,10},{10,11},{11... | collective-permute-start | bytes 152 | tf_op jit(solution)/shard_map/ppermute | solution.py:30
  173.6 1.3 collective-permute-done.14
  174.8 0.1 multiply_select_fusion.1
  175.0 7.8 %collective-permute-start.17 = (bf16[8,2,256]{2,1,0:T(2,128)(2,1)S(1)}, bf16[8,2,256]{2,1,0:T(2,128)(2,1)S(1)}, u32[]{:S(2)}, u32[]{:S(2)}) collective-permute-start(bf16[8,2,256]{2,1,0:T(2,128)(2,1)S(1)} %get-tuple-element.32), channel_id=1, source_target_pairs={{0,1},{1,2},{2,3},{3,4},{4,5},{5,6},{6,7},{8,9},{9,10},{10,11},{11... | collective-permute-start | bytes 24584 | tf_op jit(solution)/shard_map/ppermute | solution.py:30
  182.8 1.9 collective-permute-start.18
  184.7 0.7 slice_subtract_fusion.2
  185.4 6.6 %collective-permute-done.18 = bf16[8,2,256]{2,1,0:T(2,128)(2,1)S(1)} collective-permute-done((bf16[8,2,256]{2,1,0:T(2,128)(2,1)S(1)}, bf16[8,2,256]{2,1,0:T(2,128)(2,1)S(1)}, u32[]{:S(2)}, u32[]{:S(2)}) %collective-permute-start.18) | collective-permute-done | bytes 8224 | tf_op jit(solution)/shard_map/ppermute | solution.py:31
  192.0 0.2 fusion.47
  192.2 1.9 fusion.14
  194.1 0.3 broadcast_select_fusion
  194.4 1.0 fusion.23
  (57 shorter events, 0.8 us)
Async XLA Ops:
  7.2 26.5 %copy-start.1 = (bf16[4,48,256]{2,1,0:T(8,128)(2,1)S(1)}, bf16[4,48,256]{2,1,0:T(8,128)(2,1)}, u32[]{:S(2)}) copy-start(bf16[4,48,256]{2,1,0:T(8,128)(2,1)} %param.2) | copy-start | bytes 294916
  7.2 69.9 %all-gather.2.cloned.1.call-start = ((), (), s32[]{:S(2)}) async-start(), calls=%async_computation.1 | async-start | bytes 3932160 | tf_op jit(solution)/shard_map/all_gather | solution.py:167
  7.2 10.0 %collective-permute-start = (bf16[4,48,256]{2,1,0:T(8,128)(2,1)}, bf16[4,48,256]{2,1,0:T(8,128)(2,1)S(1)}, u32[]{:S(2)}, u32[]{:S(2)}) collective-permute-start(bf16[4,48,256]{2,1,0:T(8,128)(2,1)} %param.3), channel_id=1, source_target_pairs={{0,32},{32,64},{64,96},{96,128},{128,160},{160,192},{192,224},{224... | collective-permute-start | bytes 294920 | tf_op jit(solution)/shard_map/ppermute | solution.py:166
  8.3 13.8 %collective-permute-start.1 = (bf16[4,48,256]{2,1,0:T(8,128)(2,1)}, bf16[4,48,256]{2,1,0:T(8,128)(2,1)S(1)}, u32[]{:S(2)}, u32[]{:S(2)}) collective-permute-start(bf16[4,48,256]{2,1,0:T(8,128)(2,1)} %param.3), channel_id=1, source_target_pairs={{0,64},{32,96},{64,128},{96,160},{128,192},{160,224},{192,0},{224,... | collective-permute-start | bytes 294920 | tf_op jit(solution)/shard_map/ppermute | solution.py:166
  9.8 15.0 %collective-permute-start.2 = (bf16[4,48,256]{2,1,0:T(8,128)(2,1)}, bf16[4,48,256]{2,1,0:T(8,128)(2,1)S(1)}, u32[]{:S(2)}, u32[]{:S(2)}) collective-permute-start(bf16[4,48,256]{2,1,0:T(8,128)(2,1)} %param.3), channel_id=1, source_target_pairs={{0,96},{32,128},{64,160},{96,192},{128,224},{160,0},{192,32},{224,... | collective-permute-start | bytes 294920 | tf_op jit(solution)/shard_map/ppermute | solution.py:166
  9.9 14.9 %collective-permute-start.3 = (bf16[4,48,256]{2,1,0:T(8,128)(2,1)}, bf16[4,48,256]{2,1,0:T(8,128)(2,1)S(1)}, u32[]{:S(2)}, u32[]{:S(2)}) collective-permute-start(bf16[4,48,256]{2,1,0:T(8,128)(2,1)} %param.3), channel_id=1, source_target_pairs={{0,128},{32,160},{64,192},{96,224},{128,0},{160,32},{192,64},{224,... | collective-permute-start | bytes 294920 | tf_op jit(solution)/shard_map/ppermute | solution.py:166
  15.3 10.7 %collective-permute-start.4 = (bf16[4,48,256]{2,1,0:T(8,128)(2,1)}, bf16[4,48,256]{2,1,0:T(8,128)(2,1)S(1)}, u32[]{:S(2)}, u32[]{:S(2)}) collective-permute-start(bf16[4,48,256]{2,1,0:T(8,128)(2,1)} %param.3), channel_id=1, source_target_pairs={{0,160},{32,192},{64,224},{96,0},{128,32},{160,64},{192,96},{224,1... | collective-permute-start | bytes 294920 | tf_op jit(solution)/shard_map/ppermute | solution.py:166
  17.2 13.5 %collective-permute-start.5 = (bf16[4,48,256]{2,1,0:T(8,128)(2,1)}, bf16[4,48,256]{2,1,0:T(8,128)(2,1)S(1)}, u32[]{:S(2)}, u32[]{:S(2)}) collective-permute-start(bf16[4,48,256]{2,1,0:T(8,128)(2,1)} %param.3), channel_id=1, source_target_pairs={{0,192},{32,224},{64,0},{96,32},{128,64},{160,96},{192,128},{224,1... | collective-permute-start | bytes 294920 | tf_op jit(solution)/shard_map/ppermute | solution.py:166
  22.1 10.6 %collective-permute-start.6 = (bf16[4,48,256]{2,1,0:T(8,128)(2,1)}, bf16[4,48,256]{2,1,0:T(8,128)(2,1)S(1)}, u32[]{:S(2)}, u32[]{:S(2)}) collective-permute-start(bf16[4,48,256]{2,1,0:T(8,128)(2,1)} %param.3), channel_id=1, source_target_pairs={{0,224},{32,0},{64,32},{96,64},{128,96},{160,128},{192,160},{224,1... | collective-permute-start | bytes 294920 | tf_op jit(solution)/shard_map/ppermute | solution.py:166
  32.7 0.9 copy-start.2
  33.7 91.9 %collective-permute-start.7 = (bf16[2,48,256]{2,1,0:T(8,128)(2,1)S(1)}, bf16[2,48,256]{2,1,0:T(8,128)(2,1)S(1)}, u32[]{:S(2)}, u32[]{:S(2)}) collective-permute-start(bf16[2,48,256]{2,1,0:T(8,128)(2,1)S(1)} %get-tuple-element.39), channel_id=1, source_target_pairs={{0,8},{8,16},{16,24},{24,32},{32,40},{40,48},{48,56},{56,64},{64,7... | collective-permute-start | bytes 147464 | tf_op jit(solution)/shard_map/ppermute | solution.py:30
  35.6 90.0 %collective-permute-start.8 = (bf16[2,48,256]{2,1,0:T(8,128)(2,1)S(1)}, bf16[2,48,256]{2,1,0:T(8,128)(2,1)S(1)}, u32[]{:S(2)}, u32[]{:S(2)}) collective-permute-start(bf16[2,48,256]{2,1,0:T(8,128)(2,1)S(1)} %get-tuple-element.38), channel_id=1, source_target_pairs={{8,0},{16,8},{24,16},{32,24},{40,32},{48,40},{56,48},{64,56},{72,6... | collective-permute-start | bytes 147464 | tf_op jit(solution)/shard_map/ppermute | solution.py:31
  115.6 3.1 %copy-start.4 = (f32[1536,1]{1,0:T(8,128)S(1)}, f32[1536,1]{1,0:T(8,128)}, u32[]{:S(2)}) copy-start(f32[1536,1]{1,0:T(8,128)} %get-tuple-element.11) | copy-start | bytes 18436
  115.6 3.5 %copy-start.3 = (f32[1536,1]{1,0:T(8,128)S(1)}, f32[1536,1]{1,0:T(8,128)}, u32[]{:S(2)}) copy-start(f32[1536,1]{1,0:T(8,128)} %get-tuple-element.12) | copy-start | bytes 18436
  115.6 3.9 %copy-start = (f32[1536,256]{1,0:T(8,128)S(1)}, f32[1536,256]{1,0:T(8,128)}, u32[]{:S(2)}) copy-start(f32[1536,256]{1,0:T(8,128)} %get-tuple-element.8) | copy-start | bytes 4718596
  120.8 25.1 %all-to-all-start = ((f32[8,196,256]{2,1,0:T(8,128)}), f32[8,196,256]{2,1,0:T(8,128)S(1)}, u32[]{:S(2)}, u32[]{:S(2)}) async-start(f32[8,196,256]{2,1,0:T(8,128)} %select_maximum_fusion), calls=%async_computation | async-start | bytes 3276800 | tf_op jit(solution)/shard_map/all_to_all | solution.py:193
  125.7 18.4 %collective-permute-start.10 = (bf16[8,2,256]{2,1,0:T(2,128)(2,1)S(1)}, bf16[8,2,256]{2,1,0:T(2,128)(2,1)S(1)}, u32[]{:S(2)}, u32[]{:S(2)}) collective-permute-start(bf16[8,2,256]{2,1,0:T(2,128)(2,1)S(1)} %get-tuple-element.35), channel_id=1, source_target_pairs={{1,0},{2,1},{3,2},{4,3},{5,4},{6,5},{7,6},{9,8},{10,9},{11,10},{12... | collective-permute-start | bytes 24584 | tf_op jit(solution)/shard_map/ppermute | solution.py:31
  128.5 16.9 %collective-permute-start.9 = (bf16[8,2,256]{2,1,0:T(2,128)(2,1)S(1)}, bf16[8,2,256]{2,1,0:T(2,128)(2,1)S(1)}, u32[]{:S(2)}, u32[]{:S(2)}) collective-permute-start(bf16[8,2,256]{2,1,0:T(2,128)(2,1)S(1)} %get-tuple-element.34), channel_id=1, source_target_pairs={{0,1},{1,2},{2,3},{3,4},{4,5},{5,6},{6,7},{8,9},{9,10},{10,11},{11... | collective-permute-start | bytes 24584 | tf_op jit(solution)/shard_map/ppermute | solution.py:30
  147.3 27.6 %collective-permute-start.15 = (bf16[2,48,256]{2,1,0:T(8,128)(2,1)S(1)}, bf16[2,48,256]{2,1,0:T(8,128)(2,1)S(1)}, u32[]{:S(2)}, u32[]{:S(2)}) collective-permute-start(bf16[2,48,256]{2,1,0:T(8,128)(2,1)S(1)} %bitcast.37), channel_id=1, source_target_pairs={{0,8},{8,16},{16,24},{24,32},{32,40},{40,48},{48,56},{56,64},{64,7... | collective-permute-start | bytes 147464 | tf_op jit(solution)/shard_map/ppermute | solution.py:30
  149.2 25.7 %collective-permute-start.16 = (bf16[2,48,256]{2,1,0:T(8,128)(2,1)S(1)}, bf16[2,48,256]{2,1,0:T(8,128)(2,1)S(1)}, u32[]{:S(2)}, u32[]{:S(2)}) collective-permute-start(bf16[2,48,256]{2,1,0:T(8,128)(2,1)S(1)} %bitcast.36), channel_id=1, source_target_pairs={{8,0},{16,8},{24,16},{32,24},{40,32},{48,40},{56,48},{64,56},{72,6... | collective-permute-start | bytes 147464 | tf_op jit(solution)/shard_map/ppermute | solution.py:31
  155.0 4.5 %collective-permute-start.11 = (f32[2,1,48]{2,1,0:T(1,128)S(1)}, f32[2,1,48]{2,1,0:T(1,128)S(1)}, u32[]{:S(2)}, u32[]{:S(2)}) collective-permute-start(f32[2,1,48]{2,1,0:T(1,128)S(1)} %get-tuple-element.43), channel_id=1, source_target_pairs={{8,0},{16,8},{24,16},{32,24},{40,32},{48,40},{56,48},{64,56},{72,6... | collective-permute-start | bytes 1160 | tf_op jit(solution)/shard_map/ppermute | solution.py:31
  156.9 7.0 %collective-permute-start.12 = (f32[2,1,48]{2,1,0:T(1,128)S(1)}, f32[2,1,48]{2,1,0:T(1,128)S(1)}, u32[]{:S(2)}, u32[]{:S(2)}) collective-permute-start(f32[2,1,48]{2,1,0:T(1,128)S(1)} %get-tuple-element.42), channel_id=1, source_target_pairs={{0,8},{8,16},{16,24},{24,32},{32,40},{40,48},{48,56},{56,64},{64,7... | collective-permute-start | bytes 1160 | tf_op jit(solution)/shard_map/ppermute | solution.py:30
  164.0 9.5 %collective-permute-start.13 = (f32[2,6,1]{2,1,0:T(8,128)S(1)}, f32[2,6,1]{2,1,0:T(8,128)S(1)}, u32[]{:S(2)}, u32[]{:S(2)}) collective-permute-start(f32[2,6,1]{2,1,0:T(8,128)S(1)} %get-tuple-element.40), channel_id=1, source_target_pairs={{1,0},{2,1},{3,2},{4,3},{5,4},{6,5},{7,6},{9,8},{10,9},{11,10},{12... | collective-permute-start | bytes 152 | tf_op jit(solution)/shard_map/ppermute | solution.py:31
  166.9 7.9 %collective-permute-start.14 = (f32[2,6,1]{2,1,0:T(8,128)S(1)}, f32[2,6,1]{2,1,0:T(8,128)S(1)}, u32[]{:S(2)}, u32[]{:S(2)}) collective-permute-start(f32[2,6,1]{2,1,0:T(8,128)S(1)} %get-tuple-element.41), channel_id=1, source_target_pairs={{0,1},{1,2},{2,3},{3,4},{4,5},{5,6},{6,7},{8,9},{9,10},{10,11},{11... | collective-permute-start | bytes 152 | tf_op jit(solution)/shard_map/ppermute | solution.py:30
  175.0 10.4 %collective-permute-start.17 = (bf16[8,2,256]{2,1,0:T(2,128)(2,1)S(1)}, bf16[8,2,256]{2,1,0:T(2,128)(2,1)S(1)}, u32[]{:S(2)}, u32[]{:S(2)}) collective-permute-start(bf16[8,2,256]{2,1,0:T(2,128)(2,1)S(1)} %get-tuple-element.32), channel_id=1, source_target_pairs={{0,1},{1,2},{2,3},{3,4},{4,5},{5,6},{6,7},{8,9},{9,10},{10,11},{11... | collective-permute-start | bytes 24584 | tf_op jit(solution)/shard_map/ppermute | solution.py:30
  182.8 9.2 %collective-permute-start.18 = (bf16[8,2,256]{2,1,0:T(2,128)(2,1)S(1)}, bf16[8,2,256]{2,1,0:T(2,128)(2,1)S(1)}, u32[]{:S(2)}, u32[]{:S(2)}) collective-permute-start(bf16[8,2,256]{2,1,0:T(2,128)(2,1)S(1)} %get-tuple-element.33), channel_id=1, source_target_pairs={{1,0},{2,1},{3,2},{4,3},{5,4},{6,5},{7,6},{9,8},{10,9},{11,10},{12... | collective-permute-start | bytes 24584 | tf_op jit(solution)/shard_map/ppermute | solution.py:31
Sparse Core Ops, SparseCore 0:
  33.8 43.2 all-gather.1
